TPU v7x, 128 devices: a whole 4x4x4 slice. The times are simulated.
128 devices in a mesh: depth: 4 (over z_lo, core), lat: 32 (over y, z_hi, x).
Axes of the slice: x: 4, y: 4, z: 4 (z_hi: 2, z_lo: 2; z = z_hi * 2 + z_lo), core: 2. Of those that a mesh axis runs over, the one named last changes fastest.
Arguments:
- temp_old: float32 [32, 32, 256, 128], P('depth', 'lat'), may hold values from 0 to 2.5
- material: int32 [32, 32, 256, 128], P('depth', 'lat'), may hold values from 0 to 7
- conduct_table: float32 [8], replicated, may hold values from 0.3 to 3
- capacity_table: float32 [8], replicated, may hold values from 0.5 to 2
- dyn_power: float32 [4, 32, 256, 128], P('depth', 'lat'), may hold values from 0.2 to 4
- leak_ref: float32 [4, 32, 256, 128], P('depth', 'lat'), may hold values from 0.05 to 1
- die_layer: int32 [4], replicated, may hold values from 0 to 31, as said below
Outputs:
- temp_new: float32 [32, 32, 256, 128], P('depth', 'lat')
- die_power: float32 [4, 32, 256, 128], P('depth', 'lat')
Inputs may be any that keep to these rules, and one draw needn't show every extreme that they name: `die_layer`: the 4 entries name different layers of the grid; one die lies on layer 0 and one on the top layer.
All inputs are finite; a program needn't handle non-finite values.
Results may differ from a plain program's by a relative error of at most 0.000059.
Values sent between devices are 32-bit elements; how exact they have to be, the bound alone decides.
No kernel may reach another device: no remote copies, remote signals or barrier semaphores. Data moves between devices by JAX's collectives and lax.ppermute only.
A program may use at most 128 MiB of HBM per device.

v0:
```python
import functools

import jax
import jax.numpy as jnp
from jax import lax
from jax.experimental import pallas as pl
from jax.experimental.pallas import tpu as pltpu
from jax.sharding import PartitionSpec as P


SWEEPS = 6
HALO = SWEEPS
PAD_Y = 8

COND_SLOPE = 0.15
LEAK_SLOPE = 0.5
SINK_CONDUCT = 2.0

INTERPRET = False


def from_behind(block, axis, distance):
    devices = range(lax.axis_size(axis))
    route = [(i - distance, i) for i in devices if i - distance in devices]
    return lax.ppermute(block, axis, route)


def harm(a, b):
    summed = a + b
    return 2.0 * a * b / jnp.where(summed > 0, summed, 1.0)


def material_bits(material):
    hi = material >= 4.0
    rest = material - jnp.where(hi, 4.0, 0.0)
    mid = rest >= 2.0
    lo = (rest - jnp.where(mid, 2.0, 0.0)) >= 1.0
    return hi, mid, lo


def lookup(table_ref, bits):
    hi, mid, lo = bits
    t = [table_ref[i] for i in range(8)]
    low = jnp.where(mid, jnp.where(lo, t[3], t[2]), jnp.where(lo, t[1], t[0]))
    high = jnp.where(mid, jnp.where(lo, t[7], t[6]), jnp.where(lo, t[5], t[4]))
    return jnp.where(hi, high, low)


def sweep_kernel(nz, ny_total, local_depth, strip,
                 sc_ref, ctab_ref, htab_ref, tc_ref, mc_ref, xb_ref, xa_ref,
                 ylo_ref, yhi_ref, cb_ref, ca_ref, d0_ref, d1_ref, d2_ref, d3_ref,
                 out_ref, t_s, cond_s, rhs_s, inv_s, gz_s, gx_s, gxl_s, gy_s, gyu_s):
    ze = t_s.shape[1]
    ye = t_s.shape[2]
    xe = t_s.shape[3]
    g = sc_ref[0]
    s = sc_ref[1]
    z0 = g * local_depth - HALO
    row = lax.broadcasted_iota(jnp.int32, (ye, xe), 0)
    lane = lax.broadcasted_iota(jnp.int32, (ye, xe), 1)
    yg = s * strip + row - PAD_Y
    yvalid = (yg >= 0) & (yg < ny_total) & (row >= PAD_Y - HALO) & (row < PAD_Y + strip + HALO)
    top = PAD_Y + strip + HALO
    zlo = jnp.zeros((PAD_Y - HALO, xe), jnp.float32)
    zhi = jnp.zeros((ye - top, xe), jnp.float32)

    def put(dst, centre, lo, hi):
        dst[PAD_Y - HALO:PAD_Y] = lo
        dst[PAD_Y:PAD_Y + strip] = centre
        dst[PAD_Y + strip:top] = hi
        dst[0:PAD_Y - HALO] = zlo
        dst[top:ye] = zhi

    def tables(l, temp_raw, mat_raw, t_lo, t_hi, m_lo, m_hi):
        put(t_s.at[0, l], temp_raw.T, t_lo, t_hi)
        put(cond_s.at[l], mat_raw.T.astype(jnp.float32), m_lo, m_hi)
        temp = t_s[0, l]
        mat = cond_s[l]
        zg = z0 + l
        valid = yvalid & (zg >= 0) & (zg < nz)
        bits = material_bits(mat)
        cval = lookup(ctab_ref, bits)
        hval = lookup(htab_ref, bits)
        cond = jnp.where(valid, cval * jnp.exp(-COND_SLOPE * temp), 0.0)
        cond_s[l] = cond
        inv_s[l] = hval
        rhs_s[l] = hval * temp

    def below(i, c):
        tables(i, xb_ref[0, i], xb_ref[1, i], cb_ref[0, i, :HALO], cb_ref[0, i, HALO:],
               cb_ref[1, i, :HALO], cb_ref[1, i, HALO:])
        return c

    def centre(i, c):
        tables(HALO + i, tc_ref[i], mc_ref[i], ylo_ref[i], yhi_ref[i],
               ylo_ref[local_depth + i], yhi_ref[local_depth + i])
        return c

    def above(i, c):
        tables(HALO + local_depth + i, xa_ref[0, i], xa_ref[1, i], ca_ref[0, i, :HALO], ca_ref[0, i, HALO:],
               ca_ref[1, i, :HALO], ca_ref[1, i, HALO:])
        return c

    lax.fori_loop(0, HALO, below, 0)
    lax.fori_loop(0, local_depth, centre, 0)
    lax.fori_loop(0, HALO, above, 0)

    slots = (d0_ref, d1_ref, d2_ref, d3_ref)
    dies = len(slots)
    for o in range(dies):
        rel = sc_ref[2 + (g + dies - o) % dies] - z0
        relc = jnp.clip(rel, 0, ze - 1)

        @pl.when((rel >= 0) & (rel < ze))
        def _():
            rhs_s[relc] = inv_s[relc] * t_s[0, relc] + slots[o][...]

    def faces_z(l, c):
        gz_s[l] = harm(cond_s[l], cond_s[l + 1])
        return c

    lax.fori_loop(0, ze - 1, faces_z, 0)
    gz_s[ze - 1] = jnp.zeros((ye, xe), jnp.float32)

    def faces(l, c):
        cc = cond_s[l]
        gx = harm(cc, pltpu.roll(cc, xe - 1, 1))
        gx = jnp.where(lane == xe - 1, 0.0, gx)
        gy = harm(cc, pltpu.roll(cc, ye - 1, 0))
        gy = jnp.where(row == ye - 1, 0.0, gy)
        gxl = pltpu.roll(gx, 1, 1)
        gyu = pltpu.roll(gy, 1, 0)
        gx_s[l] = gx
        gxl_s[l] = gxl
        gy_s[l] = gy
        gyu_s[l] = gyu
        lm = jnp.maximum(l - 1, 0)
        gzm = jnp.where(l > 0, gz_s[lm], 0.0)
        sink = jnp.where(z0 + l == 0, SINK_CONDUCT, 0.0)
        diag = inv_s[l] + (gz_s[l] + gzm + gx + gxl + gy + gyu) + sink
        inv_s[l] = 1.0 / diag
        return c

    lax.fori_loop(1, ze - 1, faces, 0)

    def relax(src, l):
        t = t_s[src, l]
        coupled = (gz_s[l] * t_s[src, l + 1] + gz_s[l - 1] * t_s[src, l - 1]
                   + gx_s[l] * pltpu.roll(t, xe - 1, 1) + gxl_s[l] * pltpu.roll(t, 1, 1)
                   + gy_s[l] * pltpu.roll(t, ye - 1, 0) + gyu_s[l] * pltpu.roll(t, 1, 0))
        return (rhs_s[l] + coupled) * inv_s[l]

    for k in range(1, SWEEPS):
        src, dst = (k - 1) % 2, k % 2

        def body(l, c, src=src, dst=dst):
            t_s[dst, l] = relax(src, l)
            return c

        lax.fori_loop(k, ze - k, body, 0)

    last = (SWEEPS - 1) % 2

    def final(i, c):
        new = relax(last, HALO + i)
        out_ref[i] = new[PAD_Y:PAD_Y + strip].T
        return c

    lax.fori_loop(0, local_depth, final, 0)


def local_body(temp_old, material, conduct_table, capacity_table, dyn_power, leak_ref, die_layer):
    temp_start = temp_old[:, 0]
    cells_mat = material[:, 0]
    local_depth, nx, strip = temp_start.shape
    depth_n = lax.axis_size("depth")
    lat_n = lax.axis_size("lat")
    dies = dyn_power.shape[0] * depth_n
    nz = local_depth * depth_n
    g = lax.axis_index("depth")
    s = lax.axis_index("lat")
    first_layer = g * local_depth
    ye = PAD_Y + strip + HALO + (-(PAD_Y + strip + HALO)) % 8

    xb = from_behind(jnp.stack([temp_start[local_depth - HALO:],
                                cells_mat[local_depth - HALO:].astype(jnp.float32)]), "depth", 1)
    xa = from_behind(jnp.stack([temp_start[:HALO], cells_mat[:HALO].astype(jnp.float32)]), "depth", -1)

    def cols(sl):
        parts = [temp_start[:, :, sl], cells_mat[:, :, sl].astype(jnp.float32),
                 dyn_power[:, 0, :, sl], leak_ref[:, 0, :, sl]]
        return jnp.transpose(jnp.concatenate(parts), (0, 2, 1))

    nf = 2 * local_depth + 2
    ylo = from_behind(cols(slice(strip - HALO, strip)), "lat", 1)
    yhi = from_behind(cols(slice(0, HALO)), "lat", -1)

    def widen(centre, lo, hi):
        return jnp.concatenate([jnp.zeros((PAD_Y - HALO, nx), jnp.float32), lo, centre, hi,
                                jnp.zeros((ye - (PAD_Y + strip + HALO), nx), jnp.float32)])

    side = jnp.concatenate([ylo[:2 * local_depth].reshape(2, local_depth, HALO, nx),
                            yhi[:2 * local_depth].reshape(2, local_depth, HALO, nx)], axis=2)
    cb = from_behind(side[:, local_depth - HALO:], "depth", 1)
    ca = from_behind(side[:, :HALO], "depth", -1)

    def pick(die):
        at = die_layer[die] - first_layer
        atc = jnp.clip(at, 0, local_depth - 1)
        layer = widen(lax.dynamic_index_in_dim(temp_start, atc, 0, keepdims=False).T,
                      lax.dynamic_index_in_dim(ylo, atc, 0, keepdims=False),
                      lax.dynamic_index_in_dim(yhi, atc, 0, keepdims=False))
        return jnp.where((at >= 0) & (at < local_depth), layer, 0.0)

    die_temp = pick(g)
    for o in range(1, dies):
        route = [(i, (i + o) % depth_n) for i in range(depth_n)]
        die_temp = die_temp + lax.ppermute(pick((g + o) % dies), "depth", route)
    dyn_w = widen(dyn_power[0, 0].T, ylo[nf - 2], yhi[nf - 2])
    leak_w = widen(leak_ref[0, 0].T, ylo[nf - 1], yhi[nf - 1])
    power_w = dyn_w + leak_w * jnp.exp(LEAK_SLOPE * die_temp)
    die_power = power_w[PAD_Y:PAD_Y + strip].T[None]

    slots = [power_w]
    for o in range(1, dies):
        route = [(i, (i + o) % depth_n) for i in range(depth_n)]
        slots.append(lax.ppermute(power_w, "depth", route))

    sc = jnp.concatenate([jnp.stack([g, s]).astype(jnp.int32), die_layer.astype(jnp.int32)])
    ze = local_depth + 2 * HALO
    smem = pl.BlockSpec(memory_space=pltpu.MemorySpace.SMEM)
    vmem = pl.BlockSpec(memory_space=pltpu.MemorySpace.VMEM)
    full = (ze, ye, nx)
    kern = functools.partial(sweep_kernel, nz, strip * lat_n, local_depth, strip)
    out = pl.pallas_call(
        kern,
        out_shape=jax.ShapeDtypeStruct((local_depth, nx, strip), jnp.float32),
        in_specs=[smem] * 3 + [vmem] * 12,
        out_specs=vmem,
        scratch_shapes=([pltpu.VMEM((2,) + full, jnp.float32)] + [pltpu.VMEM(full, jnp.float32)] * 8),
        compiler_params=pltpu.CompilerParams(vmem_limit_bytes=60 * 1024 * 1024),
        interpret=INTERPRET,
    )(sc, conduct_table, capacity_table, temp_start, cells_mat, xb, xa, ylo, yhi, cb, ca, *slots)
    return (out[:, None], die_power[:, None])


def solution(mesh):
    return jax.shard_map(
        local_body,
        mesh=mesh,
        in_specs=(
            P("depth", "lat", None, None),
            P("depth", "lat", None, None),
            P(),
            P(),
            P("depth", "lat", None, None),
            P("depth", "lat", None, None),
            P(),
        ),
        out_specs=(P("depth", "lat", None, None), P("depth", "lat", None, None)),
        check_vma=False,
    )
```

profile of v0, /device:TPU:1, one launch (start us, length us, event | category | flops | bytes accessed | tf_op | source)
XLA Modules:
  0.0 83.6 jit_solution(16254325405028812335)
XLA Ops:
  0.6 1.6 %fusion = (f32[1,6,256,128]{3,2,1,0:T(8,128)S(1)}, f32[1,6,256,128]{3,2,1,0:T(8,128)S(1)}) fusion(s32[8,1,256,128]{3,2,0,1:T(8,128)} %bitcast.85), kind=kLoop, calls=%fused_computation.3 | loop fusion | flops 393216 | bytes 3145728 | tf_op jit(solution)/shard_map/convert_element_type | solution.py:187
  2.5 1.3 %pad_maximum_fusion = f32[2,6,256,128]{3,2,1,0:T(8,128)} fusion(f32[1,6,256,128]{3,2,1,0:T(8,128)S(1)} %get-tuple-element.15, f32[1,6,256,128]{3,2,1,0:T(8,128)S(1)} %get-tuple-element.13), kind=kLoop, calls=%fused_computation | loop fusion | flops 393216 | bytes 3145728 | tf_op jit(solution)/shard_map/stack | solution.py:185
  3.7 4.9 %collective-permute-start = (f32[2,6,256,128]{3,2,1,0:T(8,128)}, f32[2,6,256,128]{3,2,1,0:T(8,128)}, u32[]{:S(2)}, u32[]{:S(2)}) collective-permute-start(f32[2,6,256,128]{3,2,1,0:T(8,128)} %pad_maximum_fusion), channel_id=1, source_target_pairs={{0,32},{32,64},{64,96},{1,33},{33,65},{65,97},{2,34},{34,66},{66,9... | collective-permute-start | bytes 4718600 | tf_op jit(solution)/shard_map/ppermute | solution.py:25
  8.7 1.3 %pad_maximum_fusion.1 = f32[2,6,256,128]{3,2,1,0:T(8,128)} fusion(f32[1,6,256,128]{3,2,1,0:T(8,128)S(1)} %get-tuple-element.14, f32[1,6,256,128]{3,2,1,0:T(8,128)S(1)} %get-tuple-element.12), kind=kLoop, calls=%fused_computation.1 | loop fusion | flops 393216 | bytes 3145728 | tf_op jit(solution)/shard_map/stack | solution.py:187
  10.0 1.9 %collective-permute-start.1 = (f32[2,6,256,128]{3,2,1,0:T(8,128)}, f32[2,6,256,128]{3,2,1,0:T(8,128)}, u32[]{:S(2)}, u32[]{:S(2)}) collective-permute-start(f32[2,6,256,128]{3,2,1,0:T(8,128)} %pad_maximum_fusion.1), channel_id=1, source_target_pairs={{32,0},{64,32},{96,64},{33,1},{65,33},{97,65},{34,2},{66,34},{98,6... | collective-permute-start | bytes 4718600 | tf_op jit(solution)/shard_map/ppermute | solution.py:25
  12.6 0.5 copy-done.10
  13.5 3.1 %collective-permute-start.2 = (f32[18,6,256]{2,1,0:T(8,128)S(1)}, f32[18,6,256]{2,1,0:T(8,128)S(1)}, u32[]{:S(2)}, u32[]{:S(2)}) collective-permute-start(f32[18,6,256]{2,1,0:T(8,128)S(1)} %maximum_bitcast_fusion), channel_id=1, source_target_pairs={{0,1},{1,2},{2,3},{3,4},{4,5},{5,6},{6,7},{7,8},{8,9},{9,10},{10,1... | collective-permute-start | bytes 331784 | tf_op jit(solution)/shard_map/ppermute | solution.py:25
  16.6 1.3 %collective-permute-start.3 = (f32[18,6,256]{2,1,0:T(8,128)S(1)}, f32[18,6,256]{2,1,0:T(8,128)S(1)}, u32[]{:S(2)}, u32[]{:S(2)}) collective-permute-start(f32[18,6,256]{2,1,0:T(8,128)S(1)} %maximum_bitcast_fusion.1), channel_id=1, source_target_pairs={{1,0},{2,1},{3,2},{4,3},{5,4},{6,5},{7,6},{8,7},{9,8},{10,9},{11,1... | collective-permute-start | bytes 331784 | tf_op jit(solution)/shard_map/ppermute | solution.py:25
  18.0 0.6 fusion.4
  21.5 2.2 %collective-permute-done.3.yhi_ref = f32[18,6,256]{2,1,0:T(8,128)S(1)} collective-permute-done((f32[18,6,256]{2,1,0:T(8,128)S(1)}, f32[18,6,256]{2,1,0:T(8,128)S(1)}, u32[]{:S(2)}, u32[]{:S(2)}) %collective-permute-start.3) | collective-permute-done | bytes 110624 | tf_op jit(solution)/shard_map/ppermute | solution.py:25
  23.8 0.3 collective-permute-start.8
  24.2 2.2 %collective-permute-start.7 = (f32[144,256]{1,0:T(8,128)S(1)}, f32[144,256]{1,0:T(8,128)S(1)}, u32[]{:S(2)}, u32[]{:S(2)}) collective-permute-start(f32[144,256]{1,0:T(8,128)S(1)} %broadcast_select_fusion.1), channel_id=1, source_target_pairs={{0,64},{32,96},{64,0},{96,32},{1,65},{33,97},{65,1},{97,33},{2,66}... | collective-permute-start | bytes 442376 | tf_op jit(solution)/shard_map/ppermute | solution.py:218
  26.4 0.5 collective-permute-start.6
  26.9 0.6 pad_add_fusion.sc_ref
  27.8 12.1 %collective-permute-done.8 = f32[144,256]{1,0:T(8,128)S(1)} collective-permute-done((f32[144,256]{1,0:T(8,128)S(1)}, f32[144,256]{1,0:T(8,128)S(1)}, u32[]{:S(2)}, u32[]{:S(2)}) %collective-permute-start.8) | collective-permute-done | bytes 147488 | tf_op jit(solution)/shard_map/ppermute | solution.py:218
  39.8 1.9 %collective-permute-start.4 = (f32[2,6,12,256]{3,2,1,0:T(8,128)S(1)}, f32[2,6,12,256]{3,2,1,0:T(8,128)S(1)}, u32[]{:S(2)}, u32[]{:S(2)}) collective-permute-start(f32[2,6,12,256]{3,2,1,0:T(8,128)S(1)} %get-tuple-element.17), channel_id=1, source_target_pairs={{0,32},{32,64},{64,96},{1,33},{33,65},{65,97},{2,34},{34,66},{66,9... | collective-permute-start | bytes 442376 | tf_op jit(solution)/shard_map/ppermute | solution.py:25
  41.8 2.4 %collective-permute-start.5 = (f32[2,6,12,256]{3,2,1,0:T(8,128)S(1)}, f32[2,6,12,256]{3,2,1,0:T(8,128)S(1)}, u32[]{:S(2)}, u32[]{:S(2)}) collective-permute-start(f32[2,6,12,256]{3,2,1,0:T(8,128)S(1)} %get-tuple-element.16), channel_id=1, source_target_pairs={{32,0},{64,32},{96,64},{33,1},{65,33},{97,65},{34,2},{66,34},{98,6... | collective-permute-start | bytes 442376 | tf_op jit(solution)/shard_map/ppermute | solution.py:25
  44.3 1.3 %collective-permute-start.9 = (f32[144,256]{1,0:T(8,128)S(1)}, f32[144,256]{1,0:T(8,128)S(1)}, u32[]{:S(2)}, u32[]{:S(2)}) collective-permute-start(f32[144,256]{1,0:T(8,128)S(1)} %multiply_add_fusion.d0_ref), channel_id=1, source_target_pairs={{0,32},{32,64},{64,96},{96,0},{1,33},{33,65},{65,97},{97,1},{2,34}... | collective-permute-start | bytes 442376 | tf_op jit(solution)/shard_map/ppermute | solution.py:227
  45.6 5.3 %collective-permute-done.5.ca_ref = f32[2,6,12,256]{3,2,1,0:T(8,128)S(1)} collective-permute-done((f32[2,6,12,256]{3,2,1,0:T(8,128)S(1)}, f32[2,6,12,256]{3,2,1,0:T(8,128)S(1)}, u32[]{:S(2)}, u32[]{:S(2)}) %collective-permute-start.5) | collective-permute-done | bytes 147488 | tf_op jit(solution)/shard_map/ppermute | solution.py:25
  50.9 0.8 copy.28
  51.6 0.4 collective-permute-done.10.d2_ref
  52.0 3.4 %collective-permute-done.11.d3_ref = f32[144,256]{1,0:T(8,128)S(1)} collective-permute-done((f32[144,256]{1,0:T(8,128)S(1)}, f32[144,256]{1,0:T(8,128)S(1)}, u32[]{:S(2)}, u32[]{:S(2)}) %collective-permute-start.11) | collective-permute-done | bytes 147488 | tf_op jit(solution)/shard_map/ppermute | solution.py:227
  55.5 0.6 copy-done.9
  56.1 27.5 %shard_map.86 = f32[8,256,128]{2,1,0:T(8,128)} custom-call(s32[6]{0:T(128)} %pad_add_fusion.sc_ref, f32[8]{0:T(128)} %ctab_ref.1, f32[8]{0:T(128)} %htab_ref.1, f32[8,256,128]{2,1,0:T(8,128)} %bitcast.83, s32[8,256,128]{2,1,0:T(8,128)} %bitcast.86, f32[2,6,256,128]{3,2,1,0:T(8,128)} %collective-permute-done.xb_ref, ...), custom_call_target="tpu_custom_call" | custom-call | tf_op jit(solution)/shard_map/pallas_call | solution.py:235
  (65 shorter events, 2.1 us)
Async XLA Ops:
  0.6 1.7 %copy-start = (f32[8,1,256,128]{3,2,1,0:T(8,128)S(1)}, f32[8,1,256,128]{3,2,1,0:T(8,128)}, u32[]{:S(2)}) copy-start(f32[8,1,256,128]{3,2,1,0:T(8,128)} %param.7) | copy-start | bytes 3145732
  3.7 51.7 %collective-permute-start = (f32[2,6,256,128]{3,2,1,0:T(8,128)}, f32[2,6,256,128]{3,2,1,0:T(8,128)}, u32[]{:S(2)}, u32[]{:S(2)}) collective-permute-start(f32[2,6,256,128]{3,2,1,0:T(8,128)} %pad_maximum_fusion), channel_id=1, source_target_pairs={{0,32},{32,64},{64,96},{1,33},{33,65},{65,97},{2,34},{34,66},{66,9... | collective-permute-start | bytes 4718600 | tf_op jit(solution)/shard_map/ppermute | solution.py:25
  8.7 3.3 %copy-start.1 = (s32[8,1,256,128]{3,2,1,0:T(8,128)S(1)}, s32[8,1,256,128]{3,2,1,0:T(8,128)}, u32[]{:S(2)}) copy-start(s32[8,1,256,128]{3,2,1,0:T(8,128)} %param.8) | copy-start | bytes 3145732
  10.0 45.4 %collective-permute-start.1 = (f32[2,6,256,128]{3,2,1,0:T(8,128)}, f32[2,6,256,128]{3,2,1,0:T(8,128)}, u32[]{:S(2)}, u32[]{:S(2)}) collective-permute-start(f32[2,6,256,128]{3,2,1,0:T(8,128)} %pad_maximum_fusion.1), channel_id=1, source_target_pairs={{32,0},{64,32},{96,64},{33,1},{65,33},{97,65},{34,2},{66,34},{98,6... | collective-permute-start | bytes 4718600 | tf_op jit(solution)/shard_map/ppermute | solution.py:25
  12.3 0.9 %copy-start.10 = (f32[1,1,256,128]{3,2,1,0:T(8,128)S(1)}, f32[1,1,256,128]{3,2,1,0:T(8,128)}, u32[]{:S(2)}) copy-start(f32[1,1,256,128]{3,2,1,0:T(8,128)} %param.12) | copy-start | bytes 393220
  12.3 1.0 %copy-start.11 = (f32[1,1,256,128]{3,2,1,0:T(8,128)S(1)}, f32[1,1,256,128]{3,2,1,0:T(8,128)}, u32[]{:S(2)}) copy-start(f32[1,1,256,128]{3,2,1,0:T(8,128)} %param.11) | copy-start | bytes 393220
  12.3 5.7 %copy-start.12 = (s32[4]{0:T(128)S(1)}, s32[4]{0:T(128)}, u32[]{:S(2)}) copy-start(s32[4]{0:T(128)} %param.13) | copy-start | bytes 52
  13.5 8.0 %collective-permute-start.2 = (f32[18,6,256]{2,1,0:T(8,128)S(1)}, f32[18,6,256]{2,1,0:T(8,128)S(1)}, u32[]{:S(2)}, u32[]{:S(2)}) collective-permute-start(f32[18,6,256]{2,1,0:T(8,128)S(1)} %maximum_bitcast_fusion), channel_id=1, source_target_pairs={{0,1},{1,2},{2,3},{3,4},{4,5},{5,6},{6,7},{7,8},{8,9},{9,10},{10,1... | collective-permute-start | bytes 331784 | tf_op jit(solution)/shard_map/ppermute | solution.py:25
  16.6 7.1 %collective-permute-start.3 = (f32[18,6,256]{2,1,0:T(8,128)S(1)}, f32[18,6,256]{2,1,0:T(8,128)S(1)}, u32[]{:S(2)}, u32[]{:S(2)}) collective-permute-start(f32[18,6,256]{2,1,0:T(8,128)S(1)} %maximum_bitcast_fusion.1), channel_id=1, source_target_pairs={{1,0},{2,1},{3,2},{4,3},{5,4},{6,5},{7,6},{8,7},{9,8},{10,9},{11,1... | collective-permute-start | bytes 331784 | tf_op jit(solution)/shard_map/ppermute | solution.py:25
  21.5 6.2 %copy-start.3 = (f32[18,6,256]{2,1,0:T(8,128)}, f32[18,6,256]{2,1,0:T(8,128)S(1)}, u32[]{:S(2)}) copy-start(f32[18,6,256]{2,1,0:T(8,128)S(1)} %collective-permute-done.2.ylo_ref) | copy-start | bytes 331780
  23.7 4.0 %copy-start.4 = (f32[18,6,256]{2,1,0:T(8,128)}, f32[18,6,256]{2,1,0:T(8,128)S(1)}, u32[]{:S(2)}) copy-start(f32[18,6,256]{2,1,0:T(8,128)S(1)} %collective-permute-done.3.yhi_ref) | copy-start | bytes 331780
  23.8 16.1 %collective-permute-start.8 = (f32[144,256]{1,0:T(8,128)S(1)}, f32[144,256]{1,0:T(8,128)S(1)}, u32[]{:S(2)}, u32[]{:S(2)}) collective-permute-start(f32[144,256]{1,0:T(8,128)S(1)} %broadcast_select_fusion), channel_id=1, source_target_pairs={{0,96},{32,0},{64,32},{96,64},{1,97},{33,1},{65,33},{97,65},{2,98}... | collective-permute-start | bytes 442376 | tf_op jit(solution)/shard_map/ppermute | solution.py:218
  24.2 17.6 %collective-permute-start.7 = (f32[144,256]{1,0:T(8,128)S(1)}, f32[144,256]{1,0:T(8,128)S(1)}, u32[]{:S(2)}, u32[]{:S(2)}) collective-permute-start(f32[144,256]{1,0:T(8,128)S(1)} %broadcast_select_fusion.1), channel_id=1, source_target_pairs={{0,64},{32,96},{64,0},{96,32},{1,65},{33,97},{65,1},{97,33},{2,66}... | collective-permute-start | bytes 442376 | tf_op jit(solution)/shard_map/ppermute | solution.py:218
  26.4 17.8 %collective-permute-start.6 = (f32[144,256]{1,0:T(8,128)S(1)}, f32[144,256]{1,0:T(8,128)S(1)}, u32[]{:S(2)}, u32[]{:S(2)}) collective-permute-start(f32[144,256]{1,0:T(8,128)S(1)} %broadcast_select_fusion.2), channel_id=1, source_target_pairs={{0,32},{32,64},{64,96},{96,0},{1,33},{33,65},{65,97},{97,1},{2,34}... | collective-permute-start | bytes 442376 | tf_op jit(solution)/shard_map/ppermute | solution.py:218
  39.8 5.8 %collective-permute-start.4 = (f32[2,6,12,256]{3,2,1,0:T(8,128)S(1)}, f32[2,6,12,256]{3,2,1,0:T(8,128)S(1)}, u32[]{:S(2)}, u32[]{:S(2)}) collective-permute-start(f32[2,6,12,256]{3,2,1,0:T(8,128)S(1)} %get-tuple-element.17), channel_id=1, source_target_pairs={{0,32},{32,64},{64,96},{1,33},{33,65},{65,97},{2,34},{34,66},{66,9... | collective-permute-start | bytes 442376 | tf_op jit(solution)/shard_map/ppermute | solution.py:25
  41.8 9.1 %collective-permute-start.5 = (f32[2,6,12,256]{3,2,1,0:T(8,128)S(1)}, f32[2,6,12,256]{3,2,1,0:T(8,128)S(1)}, u32[]{:S(2)}, u32[]{:S(2)}) collective-permute-start(f32[2,6,12,256]{3,2,1,0:T(8,128)S(1)} %get-tuple-element.16), channel_id=1, source_target_pairs={{32,0},{64,32},{96,64},{33,1},{65,33},{97,65},{34,2},{66,34},{98,6... | collective-permute-start | bytes 442376 | tf_op jit(solution)/shard_map/ppermute | solution.py:25
  44.3 11.2 %copy-start.2 = (f32[144,256]{1,0:T(8,128)}, f32[144,256]{1,0:T(8,128)S(1)}, u32[]{:S(2)}) copy-start(f32[144,256]{1,0:T(8,128)S(1)} %multiply_add_fusion.d0_ref) | copy-start | bytes 442372
  44.3 7.4 %collective-permute-start.9 = (f32[144,256]{1,0:T(8,128)S(1)}, f32[144,256]{1,0:T(8,128)S(1)}, u32[]{:S(2)}, u32[]{:S(2)}) collective-permute-start(f32[144,256]{1,0:T(8,128)S(1)} %multiply_add_fusion.d0_ref), channel_id=1, source_target_pairs={{0,32},{32,64},{64,96},{96,0},{1,33},{33,65},{65,97},{97,1},{2,34}... | collective-permute-start | bytes 442376 | tf_op jit(solution)/shard_map/ppermute | solution.py:227
  45.6 9.9 %copy-start.5 = (f32[2,6,12,256]{3,2,1,0:T(8,128)}, f32[2,6,12,256]{3,2,1,0:T(8,128)S(1)}, u32[]{:S(2)}) copy-start(f32[2,6,12,256]{3,2,1,0:T(8,128)S(1)} %collective-permute-done.4.cb_ref) | copy-start | bytes 442372
  45.6 6.4 %collective-permute-start.10 = (f32[144,256]{1,0:T(8,128)S(1)}, f32[144,256]{1,0:T(8,128)S(1)}, u32[]{:S(2)}, u32[]{:S(2)}) collective-permute-start(f32[144,256]{1,0:T(8,128)S(1)} %multiply_add_fusion.d0_ref), channel_id=1, source_target_pairs={{0,64},{32,96},{64,0},{96,32},{1,65},{33,97},{65,1},{97,33},{2,66}... | collective-permute-start | bytes 442376 | tf_op jit(solution)/shard_map/ppermute | solution.py:227
  50.9 4.6 %copy-start.6 = (f32[2,6,12,256]{3,2,1,0:T(8,128)}, f32[2,6,12,256]{3,2,1,0:T(8,128)S(1)}, u32[]{:S(2)}) copy-start(f32[2,6,12,256]{3,2,1,0:T(8,128)S(1)} %collective-permute-done.5.ca_ref) | copy-start | bytes 442372
  50.9 4.6 %collective-permute-start.11 = (f32[144,256]{1,0:T(8,128)S(1)}, f32[144,256]{1,0:T(8,128)S(1)}, u32[]{:S(2)}, u32[]{:S(2)}) collective-permute-start(f32[144,256]{1,0:T(8,128)S(1)} %multiply_add_fusion.d0_ref), channel_id=1, source_target_pairs={{0,96},{32,0},{64,32},{96,64},{1,97},{33,1},{65,33},{97,65},{2,98}... | collective-permute-start | bytes 442376 | tf_op jit(solution)/shard_map/ppermute | solution.py:227
  51.6 3.8 %copy-start.7 = (f32[144,256]{1,0:T(8,128)}, f32[144,256]{1,0:T(8,128)S(1)}, u32[]{:S(2)}) copy-start(f32[144,256]{1,0:T(8,128)S(1)} %collective-permute-done.9.d1_ref) | copy-start | bytes 442372
  52.0 3.5 %copy-start.8 = (f32[144,256]{1,0:T(8,128)}, f32[144,256]{1,0:T(8,128)S(1)}, u32[]{:S(2)}) copy-start(f32[144,256]{1,0:T(8,128)S(1)} %collective-permute-done.10.d2_ref) | copy-start | bytes 442372
  (1 other events, 0.7 us)
where the time goes:
time: 83.9 us; the launch traced here: 83.6 us
  Pallas kernels  27.5 us (33%)
  waiting for transfers between devices  23.3 us (28%)
  starting transfers between devices  19.9 us (24%)
  other arithmetic  4.95 us (6%)
  local copies, waits for them, and re-layouts  4.39 us (5%)
  between operations  3.59 us (4%)
    pallas_call x1, Pallas kernels, local_body(): pl.pallas_call(kern, out_shape=jax.ShapeDtypeStruct((local_depth, nx, str...  27.5 us
    ppermute x6, starting transfers between devices, from_behind(): return lax.ppermute(block, axis, route)  15.6 us
    ppermute x3, waiting for transfers between devices, local_body(): die_temp = die_temp + lax.ppermute(pick((g + o) % dies), 'depth', route)  12.1 us
    ppermute x6, waiting for transfers between devices, from_behind(): return lax.ppermute(block, axis, route)  7.45 us
    ppermute x3, waiting for transfers between devices, local_body(): slots.append(lax.ppermute(power_w, 'depth', route))  3.79 us
    ppermute x3, starting transfers between devices, local_body(): die_temp = die_temp + lax.ppermute(pick((g + o) % dies), 'depth', route)  2.98 us
    unnamed x31, local copies, waits for them, and re-layouts  2.89 us
  transfers between devices with their start and end apart: 12, of which 5 were waited for; matrix products, arithmetic and copies ran while one was open for 6% of the time, Pallas kernels for 0%

commit v1 on v0

--- a/solution.py
+++ b/solution.py
@@ -201,8 +201,7 @@
 
     side = jnp.concatenate([ylo[:2 * local_depth].reshape(2, local_depth, HALO, nx),
                             yhi[:2 * local_depth].reshape(2, local_depth, HALO, nx)], axis=2)
-    cb = from_behind(side[:, local_depth - HALO:], "depth", 1)
-    ca = from_behind(side[:, :HALO], "depth", -1)
+    corner_of = {1: side[:, local_depth - HALO:], dies - 1: side[:, :HALO]}
 
     def pick(die):
         at = die_layer[die] - first_layer
@@ -213,9 +212,17 @@
         return jnp.where((at >= 0) & (at < local_depth), layer, 0.0)
 
     die_temp = pick(g)
+    got_corners = {}
     for o in range(1, dies):
         route = [(i, (i + o) % depth_n) for i in range(depth_n)]
-        die_temp = die_temp + lax.ppermute(pick((g + o) % dies), "depth", route)
+        sent = pick((g + o) % dies)
+        if o in corner_of:
+            sent = jnp.concatenate([sent, corner_of[o].reshape(-1, nx)])
+        got = lax.ppermute(sent, "depth", route)
+        die_temp = die_temp + got[:ye]
+        if o in corner_of:
+            got_corners[o] = got[ye:].reshape(2, HALO, 2 * HALO, nx)
+    cb, ca = got_corners[1], got_corners[dies - 1]
     dyn_w = widen(dyn_power[0, 0].T, ylo[nf - 2], yhi[nf - 2])
     leak_w = widen(leak_ref[0, 0].T, ylo[nf - 1], yhi[nf - 1])
     power_w = dyn_w + leak_w * jnp.exp(LEAK_SLOPE * die_temp)

time: 83.9 us -> 82.5 us (0.983)
  starting transfers between devices: 19.9 us -> 17.7 us
  local copies, waits for them, and re-layouts: 4.39 us -> 5.9 us
    ppermute x6 -> x4, waiting for transfers between devices: 7.45 us -> 2.12 us  [from_behind(): return lax.ppermute(block, axis, route)]
    ppermute x6 -> x4, starting transfers between devices: 15.6 us -> 11.2 us  [from_behind(): return lax.ppermute(block, axis, route)]
    ppermute x3, waiting for transfers between devices: 12.1 us -> 15.2 us  [local_body(): got = lax.ppermute(sent, 'depth', route)]
    ppermute x3, starting transfers between devices: 1.31 us -> 3.7 us  [local_body(): slots.append(lax.ppermute(power_w, 'depth', route))]
    reshape x0 -> x4, local copies, waits for them, and re-layouts: none -> 1.41 us  [the longest x2 1.38 us: local_body(): got_corners[o] = got[ye:].reshape(2, HALO, 2 * HALO, nx)]
    ppermute x3, waiting for transfers between devices: 3.79 us -> 5.11 us  [local_body(): slots.append(lax.ppermute(power_w, 'depth', route))]
    unnamed x31 -> x27, local copies, waits for them, and re-layouts: 2.89 us -> 2.93 us
  transfers between devices with their start and end apart: 12 -> 10, of which waited for: 5 -> 5; matrix products, arithmetic and copies ran while one was open for 6% -> 8% of each run, Pallas kernels for 0% -> 0%
where the time goes in v1:
time: 82.5 us; the launch traced here: 82.2 us
  Pallas kernels  27.5 us (33%)
  waiting for transfers between devices  22.5 us (27%)
  starting transfers between devices  17.7 us (21%)
  local copies, waits for them, and re-layouts  5.9 us (7%)
  other arithmetic  5.02 us (6%)
  between operations  3.63 us (4%)
    pallas_call x1, Pallas kernels, local_body(): pl.pallas_call(kern, out_shape=jax.ShapeDtypeStruct((local_depth, nx, str...  27.5 us
    ppermute x3, waiting for transfers between devices, local_body(): got = lax.ppermute(sent, 'depth', route)  15.2 us
    ppermute x4, starting transfers between devices, from_behind(): return lax.ppermute(block, axis, route)  11.2 us
    ppermute x3, waiting for transfers between devices, local_body(): slots.append(lax.ppermute(power_w, 'depth', route))  5.11 us
    ppermute x3, starting transfers between devices, local_body(): slots.append(lax.ppermute(power_w, 'depth', route))  3.7 us
    unnamed x27, local copies, waits for them, and re-layouts  2.93 us
    ppermute x3, starting transfers between devices, local_body(): got = lax.ppermute(sent, 'depth', route)  2.77 us
    ppermute x4, waiting for transfers between devices, from_behind(): return lax.ppermute(block, axis, route)  2.12 us
  transfers between devices with their start and end apart: 10, of which 5 were waited for; matrix products, arithmetic and copies ran while one was open for 8% of the time, Pallas kernels for 0%

profile of v1, /device:TPU:1, one launch (start us, length us, event | category | flops | bytes accessed | tf_op | source)
XLA Modules:
  0.0 82.2 jit_solution(14811314890741766604)
XLA Ops:
  0.6 1.6 %fusion = (f32[1,6,256,128]{3,2,1,0:T(8,128)S(1)}, f32[1,6,256,128]{3,2,1,0:T(8,128)S(1)}) fusion(s32[8,1,256,128]{3,2,0,1:T(8,128)} %bitcast.85), kind=kLoop, calls=%fused_computation.3 | loop fusion | flops 393216 | bytes 3145728 | tf_op jit(solution)/shard_map/convert_element_type | solution.py:187
  2.5 1.3 %pad_maximum_fusion = f32[2,6,256,128]{3,2,1,0:T(8,128)} fusion(f32[1,6,256,128]{3,2,1,0:T(8,128)S(1)} %get-tuple-element.17, f32[1,6,256,128]{3,2,1,0:T(8,128)S(1)} %get-tuple-element.15), kind=kLoop, calls=%fused_computation | loop fusion | flops 393216 | bytes 3145728 | tf_op jit(solution)/shard_map/stack | solution.py:185
  3.7 4.9 %collective-permute-start = (f32[2,6,256,128]{3,2,1,0:T(8,128)}, f32[2,6,256,128]{3,2,1,0:T(8,128)}, u32[]{:S(2)}, u32[]{:S(2)}) collective-permute-start(f32[2,6,256,128]{3,2,1,0:T(8,128)} %pad_maximum_fusion), channel_id=1, source_target_pairs={{0,32},{32,64},{64,96},{1,33},{33,65},{65,97},{2,34},{34,66},{66,9... | collective-permute-start | bytes 4718600 | tf_op jit(solution)/shard_map/ppermute | solution.py:25
  8.7 1.3 %pad_maximum_fusion.1 = f32[2,6,256,128]{3,2,1,0:T(8,128)} fusion(f32[1,6,256,128]{3,2,1,0:T(8,128)S(1)} %get-tuple-element.16, f32[1,6,256,128]{3,2,1,0:T(8,128)S(1)} %get-tuple-element.14), kind=kLoop, calls=%fused_computation.1 | loop fusion | flops 393216 | bytes 3145728 | tf_op jit(solution)/shard_map/stack | solution.py:187
  10.0 1.9 %collective-permute-start.1 = (f32[2,6,256,128]{3,2,1,0:T(8,128)}, f32[2,6,256,128]{3,2,1,0:T(8,128)}, u32[]{:S(2)}, u32[]{:S(2)}) collective-permute-start(f32[2,6,256,128]{3,2,1,0:T(8,128)} %pad_maximum_fusion.1), channel_id=1, source_target_pairs={{32,0},{64,32},{96,64},{33,1},{65,33},{97,65},{34,2},{66,34},{98,6... | collective-permute-start | bytes 4718600 | tf_op jit(solution)/shard_map/ppermute | solution.py:25
  12.6 0.5 copy-done.8
  13.5 3.1 %collective-permute-start.2 = (f32[18,6,256]{2,1,0:T(8,128)S(1)}, f32[18,6,256]{2,1,0:T(8,128)S(1)}, u32[]{:S(2)}, u32[]{:S(2)}) collective-permute-start(f32[18,6,256]{2,1,0:T(8,128)S(1)} %maximum_bitcast_fusion), channel_id=1, source_target_pairs={{0,1},{1,2},{2,3},{3,4},{4,5},{5,6},{6,7},{7,8},{8,9},{9,10},{10,1... | collective-permute-start | bytes 331784 | tf_op jit(solution)/shard_map/ppermute | solution.py:25
  16.6 1.3 %collective-permute-start.3 = (f32[18,6,256]{2,1,0:T(8,128)S(1)}, f32[18,6,256]{2,1,0:T(8,128)S(1)}, u32[]{:S(2)}, u32[]{:S(2)}) collective-permute-start(f32[18,6,256]{2,1,0:T(8,128)S(1)} %maximum_bitcast_fusion.1), channel_id=1, source_target_pairs={{1,0},{2,1},{3,2},{4,3},{5,4},{6,5},{7,6},{8,7},{9,8},{10,9},{11,1... | collective-permute-start | bytes 331784 | tf_op jit(solution)/shard_map/ppermute | solution.py:25
  18.0 0.7 fusion.9
  21.6 2.1 %collective-permute-done.3.yhi_ref = f32[18,6,256]{2,1,0:T(8,128)S(1)} collective-permute-done((f32[18,6,256]{2,1,0:T(8,128)S(1)}, f32[18,6,256]{2,1,0:T(8,128)S(1)}, u32[]{:S(2)}, u32[]{:S(2)}) %collective-permute-start.3) | collective-permute-done | bytes 110624 | tf_op jit(solution)/shard_map/ppermute | solution.py:25
  24.0 0.4 collective-permute-start.5
  24.5 2.3 %collective-permute-start.4 = (f32[288,256]{1,0:T(8,128)S(1)}, f32[288,256]{1,0:T(8,128)S(1)}, u32[]{:S(2)}, u32[]{:S(2)}) collective-permute-start(f32[288,256]{1,0:T(8,128)S(1)} %pad_maximum_fusion.2), channel_id=1, source_target_pairs={{0,32},{32,64},{64,96},{96,0},{1,33},{33,65},{65,97},{97,1},{2,34}... | collective-permute-start | bytes 884744 | tf_op jit(solution)/shard_map/ppermute | solution.py:221
  27.0 0.6 pad_add_fusion.sc_ref
  27.8 11.1 %collective-permute-done.6 = f32[144,256]{1,0:T(8,128)S(1)} collective-permute-done((f32[144,256]{1,0:T(8,128)S(1)}, f32[144,256]{1,0:T(8,128)S(1)}, u32[]{:S(2)}, u32[]{:S(2)}) %collective-permute-start.6) | collective-permute-done | bytes 147488 | tf_op jit(solution)/shard_map/ppermute | solution.py:221
  38.9 4.1 %collective-permute-done.5 = f32[288,256]{1,0:T(8,128)S(1)} collective-permute-done((f32[288,256]{1,0:T(8,128)S(1)}, f32[288,256]{1,0:T(8,128)S(1)}, u32[]{:S(2)}, u32[]{:S(2)}) %collective-permute-start.5) | collective-permute-done | bytes 294944 | tf_op jit(solution)/shard_map/ppermute | solution.py:221
  43.1 1.5 %collective-permute-start.7 = (f32[144,256]{1,0:T(8,128)S(1)}, f32[144,256]{1,0:T(8,128)S(1)}, u32[]{:S(2)}, u32[]{:S(2)}) collective-permute-start(f32[144,256]{1,0:T(8,128)S(1)} %get-tuple-element.18.d0_ref), channel_id=1, source_target_pairs={{0,32},{32,64},{64,96},{96,0},{1,33},{33,65},{65,97},{97,1},{2,34}... | collective-permute-start | bytes 442376 | tf_op jit(solution)/shard_map/ppermute | solution.py:234
  44.6 2.2 %collective-permute-start.8 = (f32[144,256]{1,0:T(8,128)S(1)}, f32[144,256]{1,0:T(8,128)S(1)}, u32[]{:S(2)}, u32[]{:S(2)}) collective-permute-start(f32[144,256]{1,0:T(8,128)S(1)} %get-tuple-element.18.d0_ref), channel_id=1, source_target_pairs={{0,64},{32,96},{64,0},{96,32},{1,65},{33,97},{65,1},{97,33},{2,66}... | collective-permute-start | bytes 442376 | tf_op jit(solution)/shard_map/ppermute | solution.py:234
  46.8 0.7 reshape.61.cb_ref
  47.5 0.7 reshape.63.ca_ref
  48.2 0.8 copy.48
  48.9 4.4 %collective-permute-done.8.d2_ref = f32[144,256]{1,0:T(8,128)S(1)} collective-permute-done((f32[144,256]{1,0:T(8,128)S(1)}, f32[144,256]{1,0:T(8,128)S(1)}, u32[]{:S(2)}, u32[]{:S(2)}) %collective-permute-start.8) | collective-permute-done | bytes 147488 | tf_op jit(solution)/shard_map/ppermute | solution.py:234
  53.4 0.7 collective-permute-done.9.d3_ref
  54.1 0.6 copy-done.7
  54.7 27.5 %shard_map.86 = f32[8,256,128]{2,1,0:T(8,128)} custom-call(s32[6]{0:T(128)} %pad_add_fusion.sc_ref, f32[8]{0:T(128)} %ctab_ref.1, f32[8]{0:T(128)} %htab_ref.1, f32[8,256,128]{2,1,0:T(8,128)} %bitcast.83, s32[8,256,128]{2,1,0:T(8,128)} %bitcast.86, f32[2,6,256,128]{3,2,1,0:T(8,128)} %collective-permute-done.xb_ref, ...), custom_call_target="tpu_custom_call" | custom-call | tf_op jit(solution)/shard_map/pallas_call | solution.py:242
  (63 shorter events, 2.3 us)
Async XLA Ops:
  0.6 1.7 %copy-start = (f32[8,1,256,128]{3,2,1,0:T(8,128)S(1)}, f32[8,1,256,128]{3,2,1,0:T(8,128)}, u32[]{:S(2)}) copy-start(f32[8,1,256,128]{3,2,1,0:T(8,128)} %param.7) | copy-start | bytes 3145732
  3.7 50.3 %collective-permute-start = (f32[2,6,256,128]{3,2,1,0:T(8,128)}, f32[2,6,256,128]{3,2,1,0:T(8,128)}, u32[]{:S(2)}, u32[]{:S(2)}) collective-permute-start(f32[2,6,256,128]{3,2,1,0:T(8,128)} %pad_maximum_fusion), channel_id=1, source_target_pairs={{0,32},{32,64},{64,96},{1,33},{33,65},{65,97},{2,34},{34,66},{66,9... | collective-permute-start | bytes 4718600 | tf_op jit(solution)/shard_map/ppermute | solution.py:25
  8.7 3.2 %copy-start.1 = (s32[8,1,256,128]{3,2,1,0:T(8,128)S(1)}, s32[8,1,256,128]{3,2,1,0:T(8,128)}, u32[]{:S(2)}) copy-start(s32[8,1,256,128]{3,2,1,0:T(8,128)} %param.8) | copy-start | bytes 3145732
  10.0 44.1 %collective-permute-start.1 = (f32[2,6,256,128]{3,2,1,0:T(8,128)}, f32[2,6,256,128]{3,2,1,0:T(8,128)}, u32[]{:S(2)}, u32[]{:S(2)}) collective-permute-start(f32[2,6,256,128]{3,2,1,0:T(8,128)} %pad_maximum_fusion.1), channel_id=1, source_target_pairs={{32,0},{64,32},{96,64},{33,1},{65,33},{97,65},{34,2},{66,34},{98,6... | collective-permute-start | bytes 4718600 | tf_op jit(solution)/shard_map/ppermute | solution.py:25
  12.3 0.9 %copy-start.8 = (f32[1,1,256,128]{3,2,1,0:T(8,128)S(1)}, f32[1,1,256,128]{3,2,1,0:T(8,128)}, u32[]{:S(2)}) copy-start(f32[1,1,256,128]{3,2,1,0:T(8,128)} %param.12) | copy-start | bytes 393220
  12.3 1.0 %copy-start.9 = (f32[1,1,256,128]{3,2,1,0:T(8,128)S(1)}, f32[1,1,256,128]{3,2,1,0:T(8,128)}, u32[]{:S(2)}) copy-start(f32[1,1,256,128]{3,2,1,0:T(8,128)} %param.11) | copy-start | bytes 393220
  12.3 5.7 %copy-start.10 = (s32[4]{0:T(128)S(1)}, s32[4]{0:T(128)}, u32[]{:S(2)}) copy-start(s32[4]{0:T(128)} %param.13) | copy-start | bytes 52
  13.5 10.3 %collective-permute-start.2 = (f32[18,6,256]{2,1,0:T(8,128)S(1)}, f32[18,6,256]{2,1,0:T(8,128)S(1)}, u32[]{:S(2)}, u32[]{:S(2)}) collective-permute-start(f32[18,6,256]{2,1,0:T(8,128)S(1)} %maximum_bitcast_fusion), channel_id=1, source_target_pairs={{0,1},{1,2},{2,3},{3,4},{4,5},{5,6},{6,7},{7,8},{8,9},{9,10},{10,1... | collective-permute-start | bytes 331784 | tf_op jit(solution)/shard_map/ppermute | solution.py:25
  16.6 7.1 %collective-permute-start.3 = (f32[18,6,256]{2,1,0:T(8,128)S(1)}, f32[18,6,256]{2,1,0:T(8,128)S(1)}, u32[]{:S(2)}, u32[]{:S(2)}) collective-permute-start(f32[18,6,256]{2,1,0:T(8,128)S(1)} %maximum_bitcast_fusion.1), channel_id=1, source_target_pairs={{1,0},{2,1},{3,2},{4,3},{5,4},{6,5},{7,6},{8,7},{9,8},{10,9},{11,1... | collective-permute-start | bytes 331784 | tf_op jit(solution)/shard_map/ppermute | solution.py:25
  23.7 0.7 copy-start.4
  23.7 0.7 copy-start.3
  24.0 19.0 %collective-permute-start.5 = (f32[288,256]{1,0:T(8,128)S(1)}, f32[288,256]{1,0:T(8,128)S(1)}, u32[]{:S(2)}, u32[]{:S(2)}) collective-permute-start(f32[288,256]{1,0:T(8,128)S(1)} %pad_maximum_fusion.3), channel_id=1, source_target_pairs={{0,96},{32,0},{64,32},{96,64},{1,97},{33,1},{65,33},{97,65},{2,98}... | collective-permute-start | bytes 884744 | tf_op jit(solution)/shard_map/ppermute | solution.py:221
  24.5 18.5 %collective-permute-start.4 = (f32[288,256]{1,0:T(8,128)S(1)}, f32[288,256]{1,0:T(8,128)S(1)}, u32[]{:S(2)}, u32[]{:S(2)}) collective-permute-start(f32[288,256]{1,0:T(8,128)S(1)} %pad_maximum_fusion.2), channel_id=1, source_target_pairs={{0,32},{32,64},{64,96},{96,0},{1,33},{33,65},{65,97},{97,1},{2,34}... | collective-permute-start | bytes 884744 | tf_op jit(solution)/shard_map/ppermute | solution.py:221
  26.8 12.0 %collective-permute-start.6 = (f32[144,256]{1,0:T(8,128)S(1)}, f32[144,256]{1,0:T(8,128)S(1)}, u32[]{:S(2)}, u32[]{:S(2)}) collective-permute-start(f32[144,256]{1,0:T(8,128)S(1)} %broadcast_select_fusion), channel_id=1, source_target_pairs={{0,64},{32,96},{64,0},{96,32},{1,65},{33,97},{65,1},{97,33},{2,66}... | collective-permute-start | bytes 442376 | tf_op jit(solution)/shard_map/ppermute | solution.py:221
  43.1 11.0 %copy-start.2 = (f32[144,256]{1,0:T(8,128)}, f32[144,256]{1,0:T(8,128)S(1)}, u32[]{:S(2)}) copy-start(f32[144,256]{1,0:T(8,128)S(1)} %get-tuple-element.18.d0_ref) | copy-start | bytes 442372
  43.1 5.8 %collective-permute-start.7 = (f32[144,256]{1,0:T(8,128)S(1)}, f32[144,256]{1,0:T(8,128)S(1)}, u32[]{:S(2)}, u32[]{:S(2)}) collective-permute-start(f32[144,256]{1,0:T(8,128)S(1)} %get-tuple-element.18.d0_ref), channel_id=1, source_target_pairs={{0,32},{32,64},{64,96},{96,0},{1,33},{33,65},{65,97},{97,1},{2,34}... | collective-permute-start | bytes 442376 | tf_op jit(solution)/shard_map/ppermute | solution.py:234
  44.6 8.8 %collective-permute-start.8 = (f32[144,256]{1,0:T(8,128)S(1)}, f32[144,256]{1,0:T(8,128)S(1)}, u32[]{:S(2)}, u32[]{:S(2)}) collective-permute-start(f32[144,256]{1,0:T(8,128)S(1)} %get-tuple-element.18.d0_ref), channel_id=1, source_target_pairs={{0,64},{32,96},{64,0},{96,32},{1,65},{33,97},{65,1},{97,33},{2,66}... | collective-permute-start | bytes 442376 | tf_op jit(solution)/shard_map/ppermute | solution.py:234
  46.8 7.3 %collective-permute-start.9 = (f32[144,256]{1,0:T(8,128)S(1)}, f32[144,256]{1,0:T(8,128)S(1)}, u32[]{:S(2)}, u32[]{:S(2)}) collective-permute-start(f32[144,256]{1,0:T(8,128)S(1)} %get-tuple-element.18.d0_ref), channel_id=1, source_target_pairs={{0,96},{32,0},{64,32},{96,64},{1,97},{33,1},{65,33},{97,65},{2,98}... | collective-permute-start | bytes 442376 | tf_op jit(solution)/shard_map/ppermute | solution.py:234
  48.9 5.1 %copy-start.5 = (f32[144,256]{1,0:T(8,128)}, f32[144,256]{1,0:T(8,128)S(1)}, u32[]{:S(2)}) copy-start(f32[144,256]{1,0:T(8,128)S(1)} %collective-permute-done.7.d1_ref) | copy-start | bytes 442372
  53.4 0.7 copy-start.6
  54.0 0.7 copy-start.7

commit v2 on v0

--- a/solution.py
+++ b/solution.py
@@ -115,15 +115,12 @@
         def _():
             rhs_s[relc] = inv_s[relc] * t_s[0, relc] + slots[o][...]
 
-    def faces_z(l, c):
-        gz_s[l] = harm(cond_s[l], cond_s[l + 1])
-        return c
-
-    lax.fori_loop(0, ze - 1, faces_z, 0)
-    gz_s[ze - 1] = jnp.zeros((ye, xe), jnp.float32)
+    gz_s[0] = harm(cond_s[0], cond_s[1])
 
     def faces(l, c):
         cc = cond_s[l]
+        gzp = harm(cc, cond_s[l + 1])
+        gz_s[l] = gzp
         gx = harm(cc, pltpu.roll(cc, xe - 1, 1))
         gx = jnp.where(lane == xe - 1, 0.0, gx)
         gy = harm(cc, pltpu.roll(cc, ye - 1, 0))
@@ -134,10 +131,8 @@
         gxl_s[l] = gxl
         gy_s[l] = gy
         gyu_s[l] = gyu
-        lm = jnp.maximum(l - 1, 0)
-        gzm = jnp.where(l > 0, gz_s[lm], 0.0)
         sink = jnp.where(z0 + l == 0, SINK_CONDUCT, 0.0)
-        diag = inv_s[l] + (gz_s[l] + gzm + gx + gxl + gy + gyu) + sink
+        diag = inv_s[l] + (gzp + gz_s[l - 1] + gx + gxl + gy + gyu) + sink
         inv_s[l] = 1.0 / diag
         return c
 

time: 83.9 us -> 83.1 us (level)
  no operation moved by 1% of the time
where the time goes in v2:
time: 83.1 us; the launch traced here: 82.8 us
  Pallas kernels  26.7 us (32%)
  waiting for transfers between devices  23.3 us (28%)
  starting transfers between devices  19.9 us (24%)
  other arithmetic  4.95 us (6%)
  local copies, waits for them, and re-layouts  4.39 us (5%)
  between operations  3.59 us (4%)
    pallas_call x1, Pallas kernels, local_body(): pl.pallas_call(kern, out_shape=jax.ShapeDtypeStruct((local_depth, nx, str...  26.7 us
    ppermute x6, starting transfers between devices, from_behind(): return lax.ppermute(block, axis, route)  15.6 us
    ppermute x3, waiting for transfers between devices, local_body(): die_temp = die_temp + lax.ppermute(pick((g + o) % dies), 'depth', route)  12.1 us
    ppermute x6, waiting for transfers between devices, from_behind(): return lax.ppermute(block, axis, route)  7.45 us
    ppermute x3, waiting for transfers between devices, local_body(): slots.append(lax.ppermute(power_w, 'depth', route))  3.79 us
    ppermute x3, starting transfers between devices, local_body(): die_temp = die_temp + lax.ppermute(pick((g + o) % dies), 'depth', route)  2.98 us
    unnamed x31, local copies, waits for them, and re-layouts  2.89 us
  transfers between devices with their start and end apart: 12, of which 5 were waited for; matrix products, arithmetic and copies ran while one was open for 6% of the time, Pallas kernels for 0%

profile of v2, /device:TPU:1, one launch (start us, length us, event | category | flops | bytes accessed | tf_op | source)
XLA Modules:
  0.0 82.8 jit_solution(3998694045334356702)
XLA Ops:
  0.6 1.6 %fusion = (f32[1,6,256,128]{3,2,1,0:T(8,128)S(1)}, f32[1,6,256,128]{3,2,1,0:T(8,128)S(1)}) fusion(s32[8,1,256,128]{3,2,0,1:T(8,128)} %bitcast.85), kind=kLoop, calls=%fused_computation.3 | loop fusion | flops 393216 | bytes 3145728 | tf_op jit(solution)/shard_map/convert_element_type | solution.py:182
  2.5 1.3 %pad_maximum_fusion = f32[2,6,256,128]{3,2,1,0:T(8,128)} fusion(f32[1,6,256,128]{3,2,1,0:T(8,128)S(1)} %get-tuple-element.15, f32[1,6,256,128]{3,2,1,0:T(8,128)S(1)} %get-tuple-element.13), kind=kLoop, calls=%fused_computation | loop fusion | flops 393216 | bytes 3145728 | tf_op jit(solution)/shard_map/stack | solution.py:180
  3.7 4.9 %collective-permute-start = (f32[2,6,256,128]{3,2,1,0:T(8,128)}, f32[2,6,256,128]{3,2,1,0:T(8,128)}, u32[]{:S(2)}, u32[]{:S(2)}) collective-permute-start(f32[2,6,256,128]{3,2,1,0:T(8,128)} %pad_maximum_fusion), channel_id=1, source_target_pairs={{0,32},{32,64},{64,96},{1,33},{33,65},{65,97},{2,34},{34,66},{66,9... | collective-permute-start | bytes 4718600 | tf_op jit(solution)/shard_map/ppermute | solution.py:25
  8.7 1.3 %pad_maximum_fusion.1 = f32[2,6,256,128]{3,2,1,0:T(8,128)} fusion(f32[1,6,256,128]{3,2,1,0:T(8,128)S(1)} %get-tuple-element.14, f32[1,6,256,128]{3,2,1,0:T(8,128)S(1)} %get-tuple-element.12), kind=kLoop, calls=%fused_computation.1 | loop fusion | flops 393216 | bytes 3145728 | tf_op jit(solution)/shard_map/stack | solution.py:182
  10.0 1.9 %collective-permute-start.1 = (f32[2,6,256,128]{3,2,1,0:T(8,128)}, f32[2,6,256,128]{3,2,1,0:T(8,128)}, u32[]{:S(2)}, u32[]{:S(2)}) collective-permute-start(f32[2,6,256,128]{3,2,1,0:T(8,128)} %pad_maximum_fusion.1), channel_id=1, source_target_pairs={{32,0},{64,32},{96,64},{33,1},{65,33},{97,65},{34,2},{66,34},{98,6... | collective-permute-start | bytes 4718600 | tf_op jit(solution)/shard_map/ppermute | solution.py:25
  12.6 0.5 copy-done.10
  13.5 3.1 %collective-permute-start.2 = (f32[18,6,256]{2,1,0:T(8,128)S(1)}, f32[18,6,256]{2,1,0:T(8,128)S(1)}, u32[]{:S(2)}, u32[]{:S(2)}) collective-permute-start(f32[18,6,256]{2,1,0:T(8,128)S(1)} %maximum_bitcast_fusion), channel_id=1, source_target_pairs={{0,1},{1,2},{2,3},{3,4},{4,5},{5,6},{6,7},{7,8},{8,9},{9,10},{10,1... | collective-permute-start | bytes 331784 | tf_op jit(solution)/shard_map/ppermute | solution.py:25
  16.6 1.3 %collective-permute-start.3 = (f32[18,6,256]{2,1,0:T(8,128)S(1)}, f32[18,6,256]{2,1,0:T(8,128)S(1)}, u32[]{:S(2)}, u32[]{:S(2)}) collective-permute-start(f32[18,6,256]{2,1,0:T(8,128)S(1)} %maximum_bitcast_fusion.1), channel_id=1, source_target_pairs={{1,0},{2,1},{3,2},{4,3},{5,4},{6,5},{7,6},{8,7},{9,8},{10,9},{11,1... | collective-permute-start | bytes 331784 | tf_op jit(solution)/shard_map/ppermute | solution.py:25
  18.0 0.6 fusion.4
  21.5 2.2 %collective-permute-done.3.yhi_ref = f32[18,6,256]{2,1,0:T(8,128)S(1)} collective-permute-done((f32[18,6,256]{2,1,0:T(8,128)S(1)}, f32[18,6,256]{2,1,0:T(8,128)S(1)}, u32[]{:S(2)}, u32[]{:S(2)}) %collective-permute-start.3) | collective-permute-done | bytes 110624 | tf_op jit(solution)/shard_map/ppermute | solution.py:25
  23.8 0.3 collective-permute-start.8
  24.2 2.2 %collective-permute-start.7 = (f32[144,256]{1,0:T(8,128)S(1)}, f32[144,256]{1,0:T(8,128)S(1)}, u32[]{:S(2)}, u32[]{:S(2)}) collective-permute-start(f32[144,256]{1,0:T(8,128)S(1)} %broadcast_select_fusion.1), channel_id=1, source_target_pairs={{0,64},{32,96},{64,0},{96,32},{1,65},{33,97},{65,1},{97,33},{2,66}... | collective-permute-start | bytes 442376 | tf_op jit(solution)/shard_map/ppermute | solution.py:213
  26.4 0.5 collective-permute-start.6
  26.9 0.6 pad_add_fusion.sc_ref
  27.8 12.1 %collective-permute-done.8 = f32[144,256]{1,0:T(8,128)S(1)} collective-permute-done((f32[144,256]{1,0:T(8,128)S(1)}, f32[144,256]{1,0:T(8,128)S(1)}, u32[]{:S(2)}, u32[]{:S(2)}) %collective-permute-start.8) | collective-permute-done | bytes 147488 | tf_op jit(solution)/shard_map/ppermute | solution.py:213
  39.8 1.9 %collective-permute-start.4 = (f32[2,6,12,256]{3,2,1,0:T(8,128)S(1)}, f32[2,6,12,256]{3,2,1,0:T(8,128)S(1)}, u32[]{:S(2)}, u32[]{:S(2)}) collective-permute-start(f32[2,6,12,256]{3,2,1,0:T(8,128)S(1)} %get-tuple-element.17), channel_id=1, source_target_pairs={{0,32},{32,64},{64,96},{1,33},{33,65},{65,97},{2,34},{34,66},{66,9... | collective-permute-start | bytes 442376 | tf_op jit(solution)/shard_map/ppermute | solution.py:25
  41.8 2.4 %collective-permute-start.5 = (f32[2,6,12,256]{3,2,1,0:T(8,128)S(1)}, f32[2,6,12,256]{3,2,1,0:T(8,128)S(1)}, u32[]{:S(2)}, u32[]{:S(2)}) collective-permute-start(f32[2,6,12,256]{3,2,1,0:T(8,128)S(1)} %get-tuple-element.16), channel_id=1, source_target_pairs={{32,0},{64,32},{96,64},{33,1},{65,33},{97,65},{34,2},{66,34},{98,6... | collective-permute-start | bytes 442376 | tf_op jit(solution)/shard_map/ppermute | solution.py:25
  44.3 1.3 %collective-permute-start.9 = (f32[144,256]{1,0:T(8,128)S(1)}, f32[144,256]{1,0:T(8,128)S(1)}, u32[]{:S(2)}, u32[]{:S(2)}) collective-permute-start(f32[144,256]{1,0:T(8,128)S(1)} %multiply_add_fusion.d0_ref), channel_id=1, source_target_pairs={{0,32},{32,64},{64,96},{96,0},{1,33},{33,65},{65,97},{97,1},{2,34}... | collective-permute-start | bytes 442376 | tf_op jit(solution)/shard_map/ppermute | solution.py:222
  45.6 5.3 %collective-permute-done.5.ca_ref = f32[2,6,12,256]{3,2,1,0:T(8,128)S(1)} collective-permute-done((f32[2,6,12,256]{3,2,1,0:T(8,128)S(1)}, f32[2,6,12,256]{3,2,1,0:T(8,128)S(1)}, u32[]{:S(2)}, u32[]{:S(2)}) %collective-permute-start.5) | collective-permute-done | bytes 147488 | tf_op jit(solution)/shard_map/ppermute | solution.py:25
  50.9 0.8 copy.28
  51.6 0.4 collective-permute-done.10.d2_ref
  52.0 3.4 %collective-permute-done.11.d3_ref = f32[144,256]{1,0:T(8,128)S(1)} collective-permute-done((f32[144,256]{1,0:T(8,128)S(1)}, f32[144,256]{1,0:T(8,128)S(1)}, u32[]{:S(2)}, u32[]{:S(2)}) %collective-permute-start.11) | collective-permute-done | bytes 147488 | tf_op jit(solution)/shard_map/ppermute | solution.py:222
  55.5 0.6 copy-done.9
  56.1 26.7 %shard_map.86 = f32[8,256,128]{2,1,0:T(8,128)} custom-call(s32[6]{0:T(128)} %pad_add_fusion.sc_ref, f32[8]{0:T(128)} %ctab_ref.1, f32[8]{0:T(128)} %htab_ref.1, f32[8,256,128]{2,1,0:T(8,128)} %bitcast.83, s32[8,256,128]{2,1,0:T(8,128)} %bitcast.86, f32[2,6,256,128]{3,2,1,0:T(8,128)} %collective-permute-done.xb_ref, ...), custom_call_target="tpu_custom_call" | custom-call | tf_op jit(solution)/shard_map/pallas_call | solution.py:230
  (65 shorter events, 2.1 us)
Async XLA Ops:
  0.6 1.7 %copy-start = (f32[8,1,256,128]{3,2,1,0:T(8,128)S(1)}, f32[8,1,256,128]{3,2,1,0:T(8,128)}, u32[]{:S(2)}) copy-start(f32[8,1,256,128]{3,2,1,0:T(8,128)} %param.7) | copy-start | bytes 3145732
  3.7 51.7 %collective-permute-start = (f32[2,6,256,128]{3,2,1,0:T(8,128)}, f32[2,6,256,128]{3,2,1,0:T(8,128)}, u32[]{:S(2)}, u32[]{:S(2)}) collective-permute-start(f32[2,6,256,128]{3,2,1,0:T(8,128)} %pad_maximum_fusion), channel_id=1, source_target_pairs={{0,32},{32,64},{64,96},{1,33},{33,65},{65,97},{2,34},{34,66},{66,9... | collective-permute-start | bytes 4718600 | tf_op jit(solution)/shard_map/ppermute | solution.py:25
  8.7 3.3 %copy-start.1 = (s32[8,1,256,128]{3,2,1,0:T(8,128)S(1)}, s32[8,1,256,128]{3,2,1,0:T(8,128)}, u32[]{:S(2)}) copy-start(s32[8,1,256,128]{3,2,1,0:T(8,128)} %param.8) | copy-start | bytes 3145732
  10.0 45.4 %collective-permute-start.1 = (f32[2,6,256,128]{3,2,1,0:T(8,128)}, f32[2,6,256,128]{3,2,1,0:T(8,128)}, u32[]{:S(2)}, u32[]{:S(2)}) collective-permute-start(f32[2,6,256,128]{3,2,1,0:T(8,128)} %pad_maximum_fusion.1), channel_id=1, source_target_pairs={{32,0},{64,32},{96,64},{33,1},{65,33},{97,65},{34,2},{66,34},{98,6... | collective-permute-start | bytes 4718600 | tf_op jit(solution)/shard_map/ppermute | solution.py:25
  12.3 0.9 %copy-start.10 = (f32[1,1,256,128]{3,2,1,0:T(8,128)S(1)}, f32[1,1,256,128]{3,2,1,0:T(8,128)}, u32[]{:S(2)}) copy-start(f32[1,1,256,128]{3,2,1,0:T(8,128)} %param.12) | copy-start | bytes 393220
  12.3 1.0 %copy-start.11 = (f32[1,1,256,128]{3,2,1,0:T(8,128)S(1)}, f32[1,1,256,128]{3,2,1,0:T(8,128)}, u32[]{:S(2)}) copy-start(f32[1,1,256,128]{3,2,1,0:T(8,128)} %param.11) | copy-start | bytes 393220
  12.3 5.7 %copy-start.12 = (s32[4]{0:T(128)S(1)}, s32[4]{0:T(128)}, u32[]{:S(2)}) copy-start(s32[4]{0:T(128)} %param.13) | copy-start | bytes 52
  13.5 8.0 %collective-permute-start.2 = (f32[18,6,256]{2,1,0:T(8,128)S(1)}, f32[18,6,256]{2,1,0:T(8,128)S(1)}, u32[]{:S(2)}, u32[]{:S(2)}) collective-permute-start(f32[18,6,256]{2,1,0:T(8,128)S(1)} %maximum_bitcast_fusion), channel_id=1, source_target_pairs={{0,1},{1,2},{2,3},{3,4},{4,5},{5,6},{6,7},{7,8},{8,9},{9,10},{10,1... | collective-permute-start | bytes 331784 | tf_op jit(solution)/shard_map/ppermute | solution.py:25
  16.6 7.1 %collective-permute-start.3 = (f32[18,6,256]{2,1,0:T(8,128)S(1)}, f32[18,6,256]{2,1,0:T(8,128)S(1)}, u32[]{:S(2)}, u32[]{:S(2)}) collective-permute-start(f32[18,6,256]{2,1,0:T(8,128)S(1)} %maximum_bitcast_fusion.1), channel_id=1, source_target_pairs={{1,0},{2,1},{3,2},{4,3},{5,4},{6,5},{7,6},{8,7},{9,8},{10,9},{11,1... | collective-permute-start | bytes 331784 | tf_op jit(solution)/shard_map/ppermute | solution.py:25
  21.5 6.2 %copy-start.3 = (f32[18,6,256]{2,1,0:T(8,128)}, f32[18,6,256]{2,1,0:T(8,128)S(1)}, u32[]{:S(2)}) copy-start(f32[18,6,256]{2,1,0:T(8,128)S(1)} %collective-permute-done.2.ylo_ref) | copy-start | bytes 331780
  23.7 4.0 %copy-start.4 = (f32[18,6,256]{2,1,0:T(8,128)}, f32[18,6,256]{2,1,0:T(8,128)S(1)}, u32[]{:S(2)}) copy-start(f32[18,6,256]{2,1,0:T(8,128)S(1)} %collective-permute-done.3.yhi_ref) | copy-start | bytes 331780
  23.8 16.1 %collective-permute-start.8 = (f32[144,256]{1,0:T(8,128)S(1)}, f32[144,256]{1,0:T(8,128)S(1)}, u32[]{:S(2)}, u32[]{:S(2)}) collective-permute-start(f32[144,256]{1,0:T(8,128)S(1)} %broadcast_select_fusion), channel_id=1, source_target_pairs={{0,96},{32,0},{64,32},{96,64},{1,97},{33,1},{65,33},{97,65},{2,98}... | collective-permute-start | bytes 442376 | tf_op jit(solution)/shard_map/ppermute | solution.py:213
  24.2 17.6 %collective-permute-start.7 = (f32[144,256]{1,0:T(8,128)S(1)}, f32[144,256]{1,0:T(8,128)S(1)}, u32[]{:S(2)}, u32[]{:S(2)}) collective-permute-start(f32[144,256]{1,0:T(8,128)S(1)} %broadcast_select_fusion.1), channel_id=1, source_target_pairs={{0,64},{32,96},{64,0},{96,32},{1,65},{33,97},{65,1},{97,33},{2,66}... | collective-permute-start | bytes 442376 | tf_op jit(solution)/shard_map/ppermute | solution.py:213
  26.4 17.8 %collective-permute-start.6 = (f32[144,256]{1,0:T(8,128)S(1)}, f32[144,256]{1,0:T(8,128)S(1)}, u32[]{:S(2)}, u32[]{:S(2)}) collective-permute-start(f32[144,256]{1,0:T(8,128)S(1)} %broadcast_select_fusion.2), channel_id=1, source_target_pairs={{0,32},{32,64},{64,96},{96,0},{1,33},{33,65},{65,97},{97,1},{2,34}... | collective-permute-start | bytes 442376 | tf_op jit(solution)/shard_map/ppermute | solution.py:213
  39.8 5.8 %collective-permute-start.4 = (f32[2,6,12,256]{3,2,1,0:T(8,128)S(1)}, f32[2,6,12,256]{3,2,1,0:T(8,128)S(1)}, u32[]{:S(2)}, u32[]{:S(2)}) collective-permute-start(f32[2,6,12,256]{3,2,1,0:T(8,128)S(1)} %get-tuple-element.17), channel_id=1, source_target_pairs={{0,32},{32,64},{64,96},{1,33},{33,65},{65,97},{2,34},{34,66},{66,9... | collective-permute-start | bytes 442376 | tf_op jit(solution)/shard_map/ppermute | solution.py:25
  41.8 9.1 %collective-permute-start.5 = (f32[2,6,12,256]{3,2,1,0:T(8,128)S(1)}, f32[2,6,12,256]{3,2,1,0:T(8,128)S(1)}, u32[]{:S(2)}, u32[]{:S(2)}) collective-permute-start(f32[2,6,12,256]{3,2,1,0:T(8,128)S(1)} %get-tuple-element.16), channel_id=1, source_target_pairs={{32,0},{64,32},{96,64},{33,1},{65,33},{97,65},{34,2},{66,34},{98,6... | collective-permute-start | bytes 442376 | tf_op jit(solution)/shard_map/ppermute | solution.py:25
  44.3 11.2 %copy-start.2 = (f32[144,256]{1,0:T(8,128)}, f32[144,256]{1,0:T(8,128)S(1)}, u32[]{:S(2)}) copy-start(f32[144,256]{1,0:T(8,128)S(1)} %multiply_add_fusion.d0_ref) | copy-start | bytes 442372
  44.3 7.4 %collective-permute-start.9 = (f32[144,256]{1,0:T(8,128)S(1)}, f32[144,256]{1,0:T(8,128)S(1)}, u32[]{:S(2)}, u32[]{:S(2)}) collective-permute-start(f32[144,256]{1,0:T(8,128)S(1)} %multiply_add_fusion.d0_ref), channel_id=1, source_target_pairs={{0,32},{32,64},{64,96},{96,0},{1,33},{33,65},{65,97},{97,1},{2,34}... | collective-permute-start | bytes 442376 | tf_op jit(solution)/shard_map/ppermute | solution.py:222
  45.6 9.9 %copy-start.5 = (f32[2,6,12,256]{3,2,1,0:T(8,128)}, f32[2,6,12,256]{3,2,1,0:T(8,128)S(1)}, u32[]{:S(2)}) copy-start(f32[2,6,12,256]{3,2,1,0:T(8,128)S(1)} %collective-permute-done.4.cb_ref) | copy-start | bytes 442372
  45.6 6.4 %collective-permute-start.10 = (f32[144,256]{1,0:T(8,128)S(1)}, f32[144,256]{1,0:T(8,128)S(1)}, u32[]{:S(2)}, u32[]{:S(2)}) collective-permute-start(f32[144,256]{1,0:T(8,128)S(1)} %multiply_add_fusion.d0_ref), channel_id=1, source_target_pairs={{0,64},{32,96},{64,0},{96,32},{1,65},{33,97},{65,1},{97,33},{2,66}... | collective-permute-start | bytes 442376 | tf_op jit(solution)/shard_map/ppermute | solution.py:222
  50.9 4.6 %copy-start.6 = (f32[2,6,12,256]{3,2,1,0:T(8,128)}, f32[2,6,12,256]{3,2,1,0:T(8,128)S(1)}, u32[]{:S(2)}) copy-start(f32[2,6,12,256]{3,2,1,0:T(8,128)S(1)} %collective-permute-done.5.ca_ref) | copy-start | bytes 442372
  50.9 4.6 %collective-permute-start.11 = (f32[144,256]{1,0:T(8,128)S(1)}, f32[144,256]{1,0:T(8,128)S(1)}, u32[]{:S(2)}, u32[]{:S(2)}) collective-permute-start(f32[144,256]{1,0:T(8,128)S(1)} %multiply_add_fusion.d0_ref), channel_id=1, source_target_pairs={{0,96},{32,0},{64,32},{96,64},{1,97},{33,1},{65,33},{97,65},{2,98}... | collective-permute-start | bytes 442376 | tf_op jit(solution)/shard_map/ppermute | solution.py:222
  51.6 3.8 %copy-start.7 = (f32[144,256]{1,0:T(8,128)}, f32[144,256]{1,0:T(8,128)S(1)}, u32[]{:S(2)}) copy-start(f32[144,256]{1,0:T(8,128)S(1)} %collective-permute-done.9.d1_ref) | copy-start | bytes 442372
  52.0 3.5 %copy-start.8 = (f32[144,256]{1,0:T(8,128)}, f32[144,256]{1,0:T(8,128)S(1)}, u32[]{:S(2)}) copy-start(f32[144,256]{1,0:T(8,128)S(1)} %collective-permute-done.10.d2_ref) | copy-start | bytes 442372
  (1 other events, 0.7 us)

commit v3 on v2

--- a/solution.py
+++ b/solution.py
@@ -124,7 +124,6 @@
         gx = harm(cc, pltpu.roll(cc, xe - 1, 1))
         gx = jnp.where(lane == xe - 1, 0.0, gx)
         gy = harm(cc, pltpu.roll(cc, ye - 1, 0))
-        gy = jnp.where(row == ye - 1, 0.0, gy)
         gxl = pltpu.roll(gx, 1, 1)
         gyu = pltpu.roll(gy, 1, 0)
         gx_s[l] = gx
@@ -152,7 +151,7 @@
             t_s[dst, l] = relax(src, l)
             return c
 
-        lax.fori_loop(k, ze - k, body, 0)
+        lax.fori_loop(k, ze - k, body, 0, unroll=2)
 
     last = (SWEEPS - 1) % 2
 
@@ -161,7 +160,7 @@
         out_ref[i] = new[PAD_Y:PAD_Y + strip].T
         return c
 
-    lax.fori_loop(0, local_depth, final, 0)
+    lax.fori_loop(0, local_depth, final, 0, unroll=2)
 
 
 def local_body(temp_old, material, conduct_table, capacity_table, dyn_power, leak_ref, die_layer):

time: 83.1 us -> 80.9 us (0.974)
  Pallas kernels: 26.7 us -> 24.5 us
    pallas_call x1, Pallas kernels: 26.7 us -> 24.5 us  [local_body(): pl.pallas_call(kern, out_shape=jax.ShapeDtypeStruct((local_depth, nx, str...]
where the time goes in v3:
time: 80.9 us; the launch traced here: 80.6 us
  Pallas kernels  24.5 us (30%)
  waiting for transfers between devices  23.3 us (29%)
  starting transfers between devices  19.9 us (25%)
  other arithmetic  4.95 us (6%)
  local copies, waits for them, and re-layouts  4.39 us (5%)
  between operations  3.59 us (4%)
    pallas_call x1, Pallas kernels, local_body(): pl.pallas_call(kern, out_shape=jax.ShapeDtypeStruct((local_depth, nx, str...  24.5 us
    ppermute x6, starting transfers between devices, from_behind(): return lax.ppermute(block, axis, route)  15.6 us
    ppermute x3, waiting for transfers between devices, local_body(): die_temp = die_temp + lax.ppermute(pick((g + o) % dies), 'depth', route)  12.1 us
    ppermute x6, waiting for transfers between devices, from_behind(): return lax.ppermute(block, axis, route)  7.45 us
    ppermute x3, waiting for transfers between devices, local_body(): slots.append(lax.ppermute(power_w, 'depth', route))  3.79 us
    ppermute x3, starting transfers between devices, local_body(): die_temp = die_temp + lax.ppermute(pick((g + o) % dies), 'depth', route)  2.98 us
    unnamed x31, local copies, waits for them, and re-layouts  2.89 us
  transfers between devices with their start and end apart: 12, of which 5 were waited for; matrix products, arithmetic and copies ran while one was open for 6% of the time, Pallas kernels for 0%

profile of v3, /device:TPU:1, one launch (start us, length us, event | category | flops | bytes accessed | tf_op | source)
XLA Modules:
  0.0 80.6 jit_solution(11987270009133982947)
XLA Ops:
  0.6 1.6 %fusion = (f32[1,6,256,128]{3,2,1,0:T(8,128)S(1)}, f32[1,6,256,128]{3,2,1,0:T(8,128)S(1)}) fusion(s32[8,1,256,128]{3,2,0,1:T(8,128)} %bitcast.85), kind=kLoop, calls=%fused_computation.3 | loop fusion | flops 393216 | bytes 3145728 | tf_op jit(solution)/shard_map/convert_element_type | solution.py:181
  2.5 1.3 %pad_maximum_fusion = f32[2,6,256,128]{3,2,1,0:T(8,128)} fusion(f32[1,6,256,128]{3,2,1,0:T(8,128)S(1)} %get-tuple-element.15, f32[1,6,256,128]{3,2,1,0:T(8,128)S(1)} %get-tuple-element.13), kind=kLoop, calls=%fused_computation | loop fusion | flops 393216 | bytes 3145728 | tf_op jit(solution)/shard_map/stack | solution.py:179
  3.7 4.9 %collective-permute-start = (f32[2,6,256,128]{3,2,1,0:T(8,128)}, f32[2,6,256,128]{3,2,1,0:T(8,128)}, u32[]{:S(2)}, u32[]{:S(2)}) collective-permute-start(f32[2,6,256,128]{3,2,1,0:T(8,128)} %pad_maximum_fusion), channel_id=1, source_target_pairs={{0,32},{32,64},{64,96},{1,33},{33,65},{65,97},{2,34},{34,66},{66,9... | collective-permute-start | bytes 4718600 | tf_op jit(solution)/shard_map/ppermute | solution.py:25
  8.7 1.3 %pad_maximum_fusion.1 = f32[2,6,256,128]{3,2,1,0:T(8,128)} fusion(f32[1,6,256,128]{3,2,1,0:T(8,128)S(1)} %get-tuple-element.14, f32[1,6,256,128]{3,2,1,0:T(8,128)S(1)} %get-tuple-element.12), kind=kLoop, calls=%fused_computation.1 | loop fusion | flops 393216 | bytes 3145728 | tf_op jit(solution)/shard_map/stack | solution.py:181
  10.0 1.9 %collective-permute-start.1 = (f32[2,6,256,128]{3,2,1,0:T(8,128)}, f32[2,6,256,128]{3,2,1,0:T(8,128)}, u32[]{:S(2)}, u32[]{:S(2)}) collective-permute-start(f32[2,6,256,128]{3,2,1,0:T(8,128)} %pad_maximum_fusion.1), channel_id=1, source_target_pairs={{32,0},{64,32},{96,64},{33,1},{65,33},{97,65},{34,2},{66,34},{98,6... | collective-permute-start | bytes 4718600 | tf_op jit(solution)/shard_map/ppermute | solution.py:25
  12.6 0.5 copy-done.10
  13.5 3.1 %collective-permute-start.2 = (f32[18,6,256]{2,1,0:T(8,128)S(1)}, f32[18,6,256]{2,1,0:T(8,128)S(1)}, u32[]{:S(2)}, u32[]{:S(2)}) collective-permute-start(f32[18,6,256]{2,1,0:T(8,128)S(1)} %maximum_bitcast_fusion), channel_id=1, source_target_pairs={{0,1},{1,2},{2,3},{3,4},{4,5},{5,6},{6,7},{7,8},{8,9},{9,10},{10,1... | collective-permute-start | bytes 331784 | tf_op jit(solution)/shard_map/ppermute | solution.py:25
  16.6 1.3 %collective-permute-start.3 = (f32[18,6,256]{2,1,0:T(8,128)S(1)}, f32[18,6,256]{2,1,0:T(8,128)S(1)}, u32[]{:S(2)}, u32[]{:S(2)}) collective-permute-start(f32[18,6,256]{2,1,0:T(8,128)S(1)} %maximum_bitcast_fusion.1), channel_id=1, source_target_pairs={{1,0},{2,1},{3,2},{4,3},{5,4},{6,5},{7,6},{8,7},{9,8},{10,9},{11,1... | collective-permute-start | bytes 331784 | tf_op jit(solution)/shard_map/ppermute | solution.py:25
  18.0 0.6 fusion.4
  21.5 2.2 %collective-permute-done.3.yhi_ref = f32[18,6,256]{2,1,0:T(8,128)S(1)} collective-permute-done((f32[18,6,256]{2,1,0:T(8,128)S(1)}, f32[18,6,256]{2,1,0:T(8,128)S(1)}, u32[]{:S(2)}, u32[]{:S(2)}) %collective-permute-start.3) | collective-permute-done | bytes 110624 | tf_op jit(solution)/shard_map/ppermute | solution.py:25
  23.8 0.3 collective-permute-start.8
  24.2 2.2 %collective-permute-start.7 = (f32[144,256]{1,0:T(8,128)S(1)}, f32[144,256]{1,0:T(8,128)S(1)}, u32[]{:S(2)}, u32[]{:S(2)}) collective-permute-start(f32[144,256]{1,0:T(8,128)S(1)} %broadcast_select_fusion.1), channel_id=1, source_target_pairs={{0,64},{32,96},{64,0},{96,32},{1,65},{33,97},{65,1},{97,33},{2,66}... | collective-permute-start | bytes 442376 | tf_op jit(solution)/shard_map/ppermute | solution.py:212
  26.4 0.5 collective-permute-start.6
  26.9 0.6 pad_add_fusion.sc_ref
  27.8 12.1 %collective-permute-done.8 = f32[144,256]{1,0:T(8,128)S(1)} collective-permute-done((f32[144,256]{1,0:T(8,128)S(1)}, f32[144,256]{1,0:T(8,128)S(1)}, u32[]{:S(2)}, u32[]{:S(2)}) %collective-permute-start.8) | collective-permute-done | bytes 147488 | tf_op jit(solution)/shard_map/ppermute | solution.py:212
  39.8 1.9 %collective-permute-start.4 = (f32[2,6,12,256]{3,2,1,0:T(8,128)S(1)}, f32[2,6,12,256]{3,2,1,0:T(8,128)S(1)}, u32[]{:S(2)}, u32[]{:S(2)}) collective-permute-start(f32[2,6,12,256]{3,2,1,0:T(8,128)S(1)} %get-tuple-element.17), channel_id=1, source_target_pairs={{0,32},{32,64},{64,96},{1,33},{33,65},{65,97},{2,34},{34,66},{66,9... | collective-permute-start | bytes 442376 | tf_op jit(solution)/shard_map/ppermute | solution.py:25
  41.8 2.4 %collective-permute-start.5 = (f32[2,6,12,256]{3,2,1,0:T(8,128)S(1)}, f32[2,6,12,256]{3,2,1,0:T(8,128)S(1)}, u32[]{:S(2)}, u32[]{:S(2)}) collective-permute-start(f32[2,6,12,256]{3,2,1,0:T(8,128)S(1)} %get-tuple-element.16), channel_id=1, source_target_pairs={{32,0},{64,32},{96,64},{33,1},{65,33},{97,65},{34,2},{66,34},{98,6... | collective-permute-start | bytes 442376 | tf_op jit(solution)/shard_map/ppermute | solution.py:25
  44.3 1.3 %collective-permute-start.9 = (f32[144,256]{1,0:T(8,128)S(1)}, f32[144,256]{1,0:T(8,128)S(1)}, u32[]{:S(2)}, u32[]{:S(2)}) collective-permute-start(f32[144,256]{1,0:T(8,128)S(1)} %multiply_add_fusion.d0_ref), channel_id=1, source_target_pairs={{0,32},{32,64},{64,96},{96,0},{1,33},{33,65},{65,97},{97,1},{2,34}... | collective-permute-start | bytes 442376 | tf_op jit(solution)/shard_map/ppermute | solution.py:221
  45.6 5.3 %collective-permute-done.5.ca_ref = f32[2,6,12,256]{3,2,1,0:T(8,128)S(1)} collective-permute-done((f32[2,6,12,256]{3,2,1,0:T(8,128)S(1)}, f32[2,6,12,256]{3,2,1,0:T(8,128)S(1)}, u32[]{:S(2)}, u32[]{:S(2)}) %collective-permute-start.5) | collective-permute-done | bytes 147488 | tf_op jit(solution)/shard_map/ppermute | solution.py:25
  50.9 0.8 copy.28
  51.6 0.4 collective-permute-done.10.d2_ref
  52.0 3.4 %collective-permute-done.11.d3_ref = f32[144,256]{1,0:T(8,128)S(1)} collective-permute-done((f32[144,256]{1,0:T(8,128)S(1)}, f32[144,256]{1,0:T(8,128)S(1)}, u32[]{:S(2)}, u32[]{:S(2)}) %collective-permute-start.11) | collective-permute-done | bytes 147488 | tf_op jit(solution)/shard_map/ppermute | solution.py:221
  55.5 0.6 copy-done.9
  56.1 24.5 %shard_map.86 = f32[8,256,128]{2,1,0:T(8,128)} custom-call(s32[6]{0:T(128)} %pad_add_fusion.sc_ref, f32[8]{0:T(128)} %ctab_ref.1, f32[8]{0:T(128)} %htab_ref.1, f32[8,256,128]{2,1,0:T(8,128)} %bitcast.83, s32[8,256,128]{2,1,0:T(8,128)} %bitcast.86, f32[2,6,256,128]{3,2,1,0:T(8,128)} %collective-permute-done.xb_ref, ...), custom_call_target="tpu_custom_call" | custom-call | tf_op jit(solution)/shard_map/pallas_call | solution.py:229
  (65 shorter events, 2.1 us)
Async XLA Ops:
  0.6 1.7 %copy-start = (f32[8,1,256,128]{3,2,1,0:T(8,128)S(1)}, f32[8,1,256,128]{3,2,1,0:T(8,128)}, u32[]{:S(2)}) copy-start(f32[8,1,256,128]{3,2,1,0:T(8,128)} %param.7) | copy-start | bytes 3145732
  3.7 51.7 %collective-permute-start = (f32[2,6,256,128]{3,2,1,0:T(8,128)}, f32[2,6,256,128]{3,2,1,0:T(8,128)}, u32[]{:S(2)}, u32[]{:S(2)}) collective-permute-start(f32[2,6,256,128]{3,2,1,0:T(8,128)} %pad_maximum_fusion), channel_id=1, source_target_pairs={{0,32},{32,64},{64,96},{1,33},{33,65},{65,97},{2,34},{34,66},{66,9... | collective-permute-start | bytes 4718600 | tf_op jit(solution)/shard_map/ppermute | solution.py:25
  8.7 3.3 %copy-start.1 = (s32[8,1,256,128]{3,2,1,0:T(8,128)S(1)}, s32[8,1,256,128]{3,2,1,0:T(8,128)}, u32[]{:S(2)}) copy-start(s32[8,1,256,128]{3,2,1,0:T(8,128)} %param.8) | copy-start | bytes 3145732
  10.0 45.4 %collective-permute-start.1 = (f32[2,6,256,128]{3,2,1,0:T(8,128)}, f32[2,6,256,128]{3,2,1,0:T(8,128)}, u32[]{:S(2)}, u32[]{:S(2)}) collective-permute-start(f32[2,6,256,128]{3,2,1,0:T(8,128)} %pad_maximum_fusion.1), channel_id=1, source_target_pairs={{32,0},{64,32},{96,64},{33,1},{65,33},{97,65},{34,2},{66,34},{98,6... | collective-permute-start | bytes 4718600 | tf_op jit(solution)/shard_map/ppermute | solution.py:25
  12.3 0.9 %copy-start.10 = (f32[1,1,256,128]{3,2,1,0:T(8,128)S(1)}, f32[1,1,256,128]{3,2,1,0:T(8,128)}, u32[]{:S(2)}) copy-start(f32[1,1,256,128]{3,2,1,0:T(8,128)} %param.12) | copy-start | bytes 393220
  12.3 1.0 %copy-start.11 = (f32[1,1,256,128]{3,2,1,0:T(8,128)S(1)}, f32[1,1,256,128]{3,2,1,0:T(8,128)}, u32[]{:S(2)}) copy-start(f32[1,1,256,128]{3,2,1,0:T(8,128)} %param.11) | copy-start | bytes 393220
  12.3 5.7 %copy-start.12 = (s32[4]{0:T(128)S(1)}, s32[4]{0:T(128)}, u32[]{:S(2)}) copy-start(s32[4]{0:T(128)} %param.13) | copy-start | bytes 52
  13.5 8.0 %collective-permute-start.2 = (f32[18,6,256]{2,1,0:T(8,128)S(1)}, f32[18,6,256]{2,1,0:T(8,128)S(1)}, u32[]{:S(2)}, u32[]{:S(2)}) collective-permute-start(f32[18,6,256]{2,1,0:T(8,128)S(1)} %maximum_bitcast_fusion), channel_id=1, source_target_pairs={{0,1},{1,2},{2,3},{3,4},{4,5},{5,6},{6,7},{7,8},{8,9},{9,10},{10,1... | collective-permute-start | bytes 331784 | tf_op jit(solution)/shard_map/ppermute | solution.py:25
  16.6 7.1 %collective-permute-start.3 = (f32[18,6,256]{2,1,0:T(8,128)S(1)}, f32[18,6,256]{2,1,0:T(8,128)S(1)}, u32[]{:S(2)}, u32[]{:S(2)}) collective-permute-start(f32[18,6,256]{2,1,0:T(8,128)S(1)} %maximum_bitcast_fusion.1), channel_id=1, source_target_pairs={{1,0},{2,1},{3,2},{4,3},{5,4},{6,5},{7,6},{8,7},{9,8},{10,9},{11,1... | collective-permute-start | bytes 331784 | tf_op jit(solution)/shard_map/ppermute | solution.py:25
  21.5 6.2 %copy-start.3 = (f32[18,6,256]{2,1,0:T(8,128)}, f32[18,6,256]{2,1,0:T(8,128)S(1)}, u32[]{:S(2)}) copy-start(f32[18,6,256]{2,1,0:T(8,128)S(1)} %collective-permute-done.2.ylo_ref) | copy-start | bytes 331780
  23.7 4.0 %copy-start.4 = (f32[18,6,256]{2,1,0:T(8,128)}, f32[18,6,256]{2,1,0:T(8,128)S(1)}, u32[]{:S(2)}) copy-start(f32[18,6,256]{2,1,0:T(8,128)S(1)} %collective-permute-done.3.yhi_ref) | copy-start | bytes 331780
  23.8 16.1 %collective-permute-start.8 = (f32[144,256]{1,0:T(8,128)S(1)}, f32[144,256]{1,0:T(8,128)S(1)}, u32[]{:S(2)}, u32[]{:S(2)}) collective-permute-start(f32[144,256]{1,0:T(8,128)S(1)} %broadcast_select_fusion), channel_id=1, source_target_pairs={{0,96},{32,0},{64,32},{96,64},{1,97},{33,1},{65,33},{97,65},{2,98}... | collective-permute-start | bytes 442376 | tf_op jit(solution)/shard_map/ppermute | solution.py:212
  24.2 17.6 %collective-permute-start.7 = (f32[144,256]{1,0:T(8,128)S(1)}, f32[144,256]{1,0:T(8,128)S(1)}, u32[]{:S(2)}, u32[]{:S(2)}) collective-permute-start(f32[144,256]{1,0:T(8,128)S(1)} %broadcast_select_fusion.1), channel_id=1, source_target_pairs={{0,64},{32,96},{64,0},{96,32},{1,65},{33,97},{65,1},{97,33},{2,66}... | collective-permute-start | bytes 442376 | tf_op jit(solution)/shard_map/ppermute | solution.py:212
  26.4 17.8 %collective-permute-start.6 = (f32[144,256]{1,0:T(8,128)S(1)}, f32[144,256]{1,0:T(8,128)S(1)}, u32[]{:S(2)}, u32[]{:S(2)}) collective-permute-start(f32[144,256]{1,0:T(8,128)S(1)} %broadcast_select_fusion.2), channel_id=1, source_target_pairs={{0,32},{32,64},{64,96},{96,0},{1,33},{33,65},{65,97},{97,1},{2,34}... | collective-permute-start | bytes 442376 | tf_op jit(solution)/shard_map/ppermute | solution.py:212
  39.8 5.8 %collective-permute-start.4 = (f32[2,6,12,256]{3,2,1,0:T(8,128)S(1)}, f32[2,6,12,256]{3,2,1,0:T(8,128)S(1)}, u32[]{:S(2)}, u32[]{:S(2)}) collective-permute-start(f32[2,6,12,256]{3,2,1,0:T(8,128)S(1)} %get-tuple-element.17), channel_id=1, source_target_pairs={{0,32},{32,64},{64,96},{1,33},{33,65},{65,97},{2,34},{34,66},{66,9... | collective-permute-start | bytes 442376 | tf_op jit(solution)/shard_map/ppermute | solution.py:25
  41.8 9.1 %collective-permute-start.5 = (f32[2,6,12,256]{3,2,1,0:T(8,128)S(1)}, f32[2,6,12,256]{3,2,1,0:T(8,128)S(1)}, u32[]{:S(2)}, u32[]{:S(2)}) collective-permute-start(f32[2,6,12,256]{3,2,1,0:T(8,128)S(1)} %get-tuple-element.16), channel_id=1, source_target_pairs={{32,0},{64,32},{96,64},{33,1},{65,33},{97,65},{34,2},{66,34},{98,6... | collective-permute-start | bytes 442376 | tf_op jit(solution)/shard_map/ppermute | solution.py:25
  44.3 11.2 %copy-start.2 = (f32[144,256]{1,0:T(8,128)}, f32[144,256]{1,0:T(8,128)S(1)}, u32[]{:S(2)}) copy-start(f32[144,256]{1,0:T(8,128)S(1)} %multiply_add_fusion.d0_ref) | copy-start | bytes 442372
  44.3 7.4 %collective-permute-start.9 = (f32[144,256]{1,0:T(8,128)S(1)}, f32[144,256]{1,0:T(8,128)S(1)}, u32[]{:S(2)}, u32[]{:S(2)}) collective-permute-start(f32[144,256]{1,0:T(8,128)S(1)} %multiply_add_fusion.d0_ref), channel_id=1, source_target_pairs={{0,32},{32,64},{64,96},{96,0},{1,33},{33,65},{65,97},{97,1},{2,34}... | collective-permute-start | bytes 442376 | tf_op jit(solution)/shard_map/ppermute | solution.py:221
  45.6 9.9 %copy-start.5 = (f32[2,6,12,256]{3,2,1,0:T(8,128)}, f32[2,6,12,256]{3,2,1,0:T(8,128)S(1)}, u32[]{:S(2)}) copy-start(f32[2,6,12,256]{3,2,1,0:T(8,128)S(1)} %collective-permute-done.4.cb_ref) | copy-start | bytes 442372
  45.6 6.4 %collective-permute-start.10 = (f32[144,256]{1,0:T(8,128)S(1)}, f32[144,256]{1,0:T(8,128)S(1)}, u32[]{:S(2)}, u32[]{:S(2)}) collective-permute-start(f32[144,256]{1,0:T(8,128)S(1)} %multiply_add_fusion.d0_ref), channel_id=1, source_target_pairs={{0,64},{32,96},{64,0},{96,32},{1,65},{33,97},{65,1},{97,33},{2,66}... | collective-permute-start | bytes 442376 | tf_op jit(solution)/shard_map/ppermute | solution.py:221
  50.9 4.6 %copy-start.6 = (f32[2,6,12,256]{3,2,1,0:T(8,128)}, f32[2,6,12,256]{3,2,1,0:T(8,128)S(1)}, u32[]{:S(2)}) copy-start(f32[2,6,12,256]{3,2,1,0:T(8,128)S(1)} %collective-permute-done.5.ca_ref) | copy-start | bytes 442372
  50.9 4.6 %collective-permute-start.11 = (f32[144,256]{1,0:T(8,128)S(1)}, f32[144,256]{1,0:T(8,128)S(1)}, u32[]{:S(2)}, u32[]{:S(2)}) collective-permute-start(f32[144,256]{1,0:T(8,128)S(1)} %multiply_add_fusion.d0_ref), channel_id=1, source_target_pairs={{0,96},{32,0},{64,32},{96,64},{1,97},{33,1},{65,33},{97,65},{2,98}... | collective-permute-start | bytes 442376 | tf_op jit(solution)/shard_map/ppermute | solution.py:221
  51.6 3.8 %copy-start.7 = (f32[144,256]{1,0:T(8,128)}, f32[144,256]{1,0:T(8,128)S(1)}, u32[]{:S(2)}) copy-start(f32[144,256]{1,0:T(8,128)S(1)} %collective-permute-done.9.d1_ref) | copy-start | bytes 442372
  52.0 3.5 %copy-start.8 = (f32[144,256]{1,0:T(8,128)}, f32[144,256]{1,0:T(8,128)S(1)}, u32[]{:S(2)}) copy-start(f32[144,256]{1,0:T(8,128)S(1)} %collective-permute-done.10.d2_ref) | copy-start | bytes 442372
  (1 other events, 0.7 us)
